TPU v7x, 32 devices: a whole 2x2x4 slice. The times are simulated.
32 devices in a mesh: grp: 2 (over y), ctx: 2 (over core), tp: 8 (over z, x).
Axes of the slice: x: 2, y: 2, z: 4, core: 2. Of those that a mesh axis runs over, the one named last changes fastest.
Arguments:
- queries: bfloat16 [8192, 8, 192], P(('grp', 'ctx'), 'tp'), parts along dimension 0, may hold values from -70 to 70
- latent_rows: bfloat16 [8192, 576], P(('grp', 'ctx', 'tp')), parts along dimension 0, may hold values from -6 to 6
- doc_ids: int32 [8192], P(('grp', 'ctx', 'tp')), parts along dimension 0, may hold values from 0 to 7, as said below
- key_weight: bfloat16 [512, 1024], P(None, 'tp'), may hold values from -0.25 to 0.25
- value_weight: bfloat16 [512, 1024], P(None, 'tp'), may hold values from -0.25 to 0.25
Outputs:
- attended: bfloat16 [8192, 1024], P(('grp', 'ctx'), 'tp'), parts along dimension 0
There are 2 independent parts, one for each index of `grp`. A program takes and returns all parts, laid end to end along the dimension named above; an argument that names none is the same for every part. Nothing has to cross between parts.
Inputs may be any that keep to these rules, and one draw needn't show every extreme that they name: `doc_ids`: never falling along the tokens.
All inputs are finite; a program needn't handle non-finite values.
Results may differ from a plain program's by a relative error of at most 0.0065.
Values may be sent and summed in bfloat16 or wider, within the bound.
No kernel may reach another device: no remote copies, remote signals or barrier semaphores. Data moves between devices by JAX's collectives and lax.ppermute only.
A program may use at most 64 MiB of HBM per device.

v0:
```python
import functools
import math

import jax
import jax.numpy as jnp
import numpy as np
from jax import lax
from jax.experimental import pallas as pl
from jax.experimental.pallas import tpu as pltpu
from jax.sharding import PartitionSpec as P

KV_RANK = 512
ROPE_DIM = 64
NOPE_DIM = 128
LANES = 128
BLOCK_Q = 512
BLOCK_K = 512
FAR = 1 << 30


def flash_kernel(
    qbase_ref, kminp_ref, kmaxp_ref, kmind_ref, kmaxd_ref,
    q_ref, *rest, sets, tiles, factor,
):
    set_refs = [rest[4 * n : 4 * n + 4] for n in range(sets)]
    o_ref = rest[4 * sets]
    qt = pl.program_id(1)
    bq = q_ref.shape[0]
    bk = BLOCK_K
    first_pos = qbase_ref[0] + qt * bq
    last_pos = first_pos + (bq - 1)
    own = (sets - 1) * tiles + qt
    first_doc = kmind_ref[own]
    last_doc = kmaxd_ref[own]
    q = q_ref[...]
    q_nope = q[:, :NOPE_DIM]
    q_rope = q[:, NOPE_DIM:]
    q_pos = first_pos + lax.broadcasted_iota(jnp.int32, (bq, 1), 0)
    q_doc = set_refs[-1][2][pl.ds(pl.multiple_of(qt * bq, bq), bq), :][:, ROPE_DIM : ROPE_DIM + 1].astype(jnp.float32)
    nt = (((1,), (1,)), ((), ()))

    m_sc, l_sc, acc_sc = rest[4 * sets + 1 :]
    m_sc[...] = jnp.full(m_sc.shape, -1e30, jnp.float32)
    l_sc[...] = jnp.zeros(l_sc.shape, jnp.float32)
    acc_sc[...] = jnp.zeros(acc_sc.shape, jnp.float32)

    def make_step(number, k_ref, v_ref, r_ref, kp_ref):
        def tile(masked, t):
            start = pl.multiple_of(t * bk, bk)
            keys = k_ref[pl.ds(start, bk), :]
            ropes = r_ref[pl.ds(start, bk), :]
            scores = lax.dot_general(q_nope, keys, nt, preferred_element_type=jnp.float32)
            scores = scores + lax.dot_general(
                q_rope, ropes[:, :ROPE_DIM], nt, preferred_element_type=jnp.float32
            )
            scores = scores * factor
            if masked:
                k_pos = kp_ref[:, pl.ds(start, bk)]
                k_doc = jnp.transpose(ropes.astype(jnp.float32))[ROPE_DIM : ROPE_DIM + 1, :]
                visible = (k_pos <= q_pos) & (k_doc == q_doc)
                scores = jnp.where(visible, scores, jnp.float32(-1e30))
            m_prev = m_sc[...]
            m_new = jnp.maximum(m_prev, jnp.max(scores, axis=1, keepdims=True))
            alpha = jnp.exp(m_prev - m_new)
            weights = jnp.exp(scores - m_new)
            l_sc[...] = alpha * l_sc[...] + jnp.sum(weights, axis=1, keepdims=True)
            acc_sc[...] = alpha * acc_sc[...] + jnp.dot(
                weights.astype(jnp.bfloat16),
                v_ref[pl.ds(start, bk), :],
                preferred_element_type=jnp.float32,
            )
            m_sc[...] = m_new

        def step(t, carry):
            at = number * tiles + t
            active = (
                (kminp_ref[at] <= last_pos)
                & (kmaxd_ref[at] >= first_doc)
                & (kmind_ref[at] <= last_doc)
            )
            full = (
                (kmaxp_ref[at] <= first_pos)
                & (kmind_ref[at] == last_doc)
                & (kmaxd_ref[at] == first_doc)
            )

            @pl.when(active & full)
            def _():
                tile(False, t)

            @pl.when(active & jnp.logical_not(full))
            def _():
                tile(True, t)

            return carry

        return step

    for number, refs in enumerate(set_refs):
        lax.fori_loop(0, tiles, make_step(number, *refs), 0)
    o_ref[...] = (acc_sc[...] / l_sc[...]).astype(o_ref.dtype)


def flash(query_heads, packs, positions, pos_tables, doc_ends, query_base):
    heads_here, rows, _ = query_heads.shape
    count = packs[0].shape[0]
    bq = min(BLOCK_Q, rows)
    bk = BLOCK_K
    q_tiles = rows // bq
    tiles = count // bk
    sets = len(packs)
    assert bq == bk and rows == count
    kminp, kmaxp = pos_tables
    kmind = jnp.concatenate([ends[0] for ends in doc_ends], axis=0)
    kmaxd = jnp.concatenate([ends[1] for ends in doc_ends], axis=0)

    in_specs = [pl.BlockSpec((None, bq, query_heads.shape[2]), lambda h, qt, *_: (h, qt, 0))]
    operands = [query_heads]
    for pack, pos in zip(packs, positions):
        in_specs += [
            pl.BlockSpec((count, LANES), lambda h, qt, *_: (0, h)),
            pl.BlockSpec((count, LANES), lambda h, qt, *_: (0, heads_here + h)),
            pl.BlockSpec((count, LANES), lambda h, qt, *_: (0, 2 * heads_here)),
            pl.BlockSpec((1, count), lambda h, qt, *_: (0, 0)),
        ]
        operands += [pack, pack, pack, pos]

    kernel = functools.partial(
        flash_kernel, sets=sets, tiles=tiles, factor=1.0 / math.sqrt(NOPE_DIM + ROPE_DIM)
    )
    grid_spec = pltpu.PrefetchScalarGridSpec(
        num_scalar_prefetch=5,
        grid=(heads_here, q_tiles),
        in_specs=in_specs,
        out_specs=pl.BlockSpec((bq, LANES), lambda h, qt, *_: (qt, h)),
        scratch_shapes=[
            pltpu.VMEM((bq, 1), jnp.float32),
            pltpu.VMEM((bq, 1), jnp.float32),
            pltpu.VMEM((bq, LANES), jnp.float32),
        ],
    )
    return pl.pallas_call(
        kernel,
        grid_spec=grid_spec,
        out_shape=jax.ShapeDtypeStruct((rows, heads_here * LANES), jnp.bfloat16),
        compiler_params=pltpu.CompilerParams(dimension_semantics=("arbitrary", "arbitrary")),
    )(query_base, kminp, kmaxp, kmind, kmaxd, *operands)


def ring_tables(order):
    count = len(order)
    place = {device: number for number, device in enumerate(order)}
    ahead = count // 2
    behind = count - 1 - ahead
    sources = [list(range(count))]
    for step in range(1, ahead + 1):
        sources.append([order[(place[d] - step) % count] for d in range(count)])
        if step <= behind:
            sources.append([order[(place[d] + step) % count] for d in range(count)])
    source_of = np.zeros((count, count), np.int32)
    slot_of = np.zeros((count, count), np.int32)
    for number, row in enumerate(sources):
        for device, source in enumerate(row):
            source_of[device, number] = source
            slot_of[device, source] = number
    me = lax.axis_index("tp")
    return jnp.asarray(source_of)[me], jnp.asarray(slot_of)[me]


def ring_gather(block, order, early, source_of):
    count = len(order)
    place = {device: number for number, device in enumerate(order)}
    forward = [(order[i], order[(i + 1) % count]) for i in range(count)]
    backward = [(order[(i + 1) % count], order[i]) for i in range(count)]
    ahead = count // 2
    behind = count - 1 - ahead
    arrived = [block]
    moving_f = block
    moving_b = block
    for step in range(1, ahead + 1):
        moving_f = lax.ppermute(moving_f, "tp", forward)
        if step <= behind:
            moving_b = lax.ppermute(moving_b, "tp", backward)
        if step == 1:
            moving_f, moving_b, early = lax.optimization_barrier((moving_f, moving_b, early))
        arrived.append(moving_f)
        if step <= behind:
            arrived.append(moving_b)
    rows = block.shape[0]
    placed = jnp.zeros((count * rows, block.shape[1]), block.dtype)
    for number, piece in enumerate(arrived):
        placed = lax.dynamic_update_slice(placed, piece, (source_of[number] * rows, 0))
    return placed, early


def body(queries, latent_rows, doc_ids, key_weight, value_weight, *, order):
    block_rows = queries.shape[0]
    chunk_rows = latent_rows.shape[0]
    chunks = block_rows // chunk_rows
    cycle_size = lax.axis_size("ctx")
    cycle_index = lax.axis_index("ctx")
    heads_here = key_weight.shape[1] // NOPE_DIM
    width = latent_rows.shape[1]
    pad = (-(width + 1)) % LANES
    doc_column = jnp.concatenate(
        [doc_ids.astype(jnp.bfloat16)[:, None], jnp.zeros((chunk_rows, pad), jnp.bfloat16)],
        axis=1,
    )
    chunk = jnp.concatenate([latent_rows, doc_column], axis=1)
    source_of, slot_of = ring_tables(order)
    offsets = jnp.arange(block_rows, dtype=jnp.int32)
    positions = []
    for distance in range(cycle_size - 1, 0, -1):
        source = cycle_index - distance
        positions.append(jnp.where(source >= 0, source * block_rows + offsets, FAR))
    positions.append(cycle_index * block_rows + offsets)
    pos_tiles = jnp.concatenate(positions, axis=0).reshape(-1, BLOCK_K)
    pos_tables = (jnp.min(pos_tiles, axis=1), jnp.max(pos_tiles, axis=1))
    query_base = (cycle_index * block_rows).astype(jnp.int32).reshape(1)
    query_heads = jnp.transpose(queries, (1, 0, 2))
    early = (tuple(pos.reshape(1, -1) for pos in positions), pos_tables, query_base, query_heads)
    gathered, early = ring_gather(chunk, order, early, source_of)
    positions, pos_tables, query_base, query_heads = early
    latent_part = gathered[:, :KV_RANK]
    key_heads = jnp.dot(latent_part, key_weight, preferred_element_type=jnp.float32).astype(
        jnp.bfloat16
    )
    value_heads = jnp.dot(latent_part, value_weight, preferred_element_type=jnp.float32).astype(
        jnp.bfloat16
    )
    pack = jnp.concatenate([key_heads, value_heads, gathered[:, KV_RANK:]], axis=1)
    doc_at = 2 * heads_here * NOPE_DIM + ROPE_DIM

    def ends_of(source):
        return (
            source[::BLOCK_K, doc_at].astype(jnp.int32),
            source[BLOCK_K - 1 :: BLOCK_K, doc_at].astype(jnp.int32),
        )

    packs, doc_ends = [], []
    for distance in range(cycle_size - 1, 0, -1):
        route = [(i - distance, i) for i in range(cycle_size) if i - distance >= 0]
        moved = lax.ppermute(pack, "ctx", route)
        packs.append(moved)
        doc_ends.append(ends_of(moved))
    packs.append(pack)
    doc_ends.append(ends_of(pack))
    return flash(query_heads, packs, positions, pos_tables, doc_ends, query_base)


def ring_order(mesh):
    line = list(mesh.devices[(0,) * (mesh.devices.ndim - 1)].reshape(-1))
    try:
        where = {(d.coords[0], d.coords[2]): number for number, d in enumerate(line)}
        xs = sorted({key[0] for key in where})
        zs = sorted({key[1] for key in where})
        order = []
        for turn, x in enumerate(xs):
            for z in zs if turn % 2 == 0 else zs[::-1]:
                order.append(where[(x, z)])
    except (AttributeError, KeyError, IndexError, TypeError):
        return list(range(len(line)))
    if sorted(order) != list(range(len(line))):
        return list(range(len(line)))
    return order


def solution(mesh):
    placed = (
        P(("grp", "ctx"), "tp", None),
        P(("grp", "ctx", "tp"), None),
        P(("grp", "ctx", "tp")),
        P(None, "tp"),
        P(None, "tp"),
    )
    return jax.shard_map(
        functools.partial(body, order=ring_order(mesh)),
        mesh=mesh,
        in_specs=placed,
        out_specs=P(("grp", "ctx"), "tp"),
        check_vma=False,
    )
```

profile of v0, /device:TPU:1, one launch (start us, length us, event | category | flops | bytes accessed | tf_op | source)
XLA Modules:
  0.0 66.9 jit_solution(14047542875002953836)
XLA Ops:
  0.0 0.0 copy-start
  0.0 0.7 %constant_dynamic-slice_fusion = s32[1,8]{1,0:T(1,128)S(1)} fusion(s32[8,8]{1,0:T(8,128)} %constant.42.clone, s32[]{:T(128)S(6)} %select_n.51), kind=kLoop, calls=%fused_computation.22 | loop fusion | bytes 68 | tf_op jit(solution)/shard_map/dynamic_slice | solution.py:167
  0.7 0.7 fusion.5
  2.0 1.2 %copy.16 = bf16[256,576]{1,0:T(8,128)(2,1)S(1)} copy(bf16[256,576]{0,1:T(8,128)(2,1)} %param.7) | data formatting | bytes 589824 | tf_op args[1]
  3.2 0.7 %convert_element_type.25 = bf16[256]{0:T(256)(128)(2,1)S(1)} convert(s32[256]{0:T(256)} %param.8) | non-fusion elementwise | flops 256 | bytes 1536 | tf_op jit(solution)/shard_map/convert_element_type | solution.py:206
  3.9 0.1 broadcast_in_dim.20
  4.0 0.1 pad.11.clone
  4.1 0.2 broadcast_in_dim.19
  4.3 0.8 %constant_dynamic-update-slice_fusion.7 = (bf16[2048,640]{1,0:T(8,128)(2,1)S(1)}, bf16[256,640]{1,0:T(8,128)(2,1)}) fusion(bf16[2048,640]{1,0:T(8,128)(2,1)S(1)} %broadcast_in_dim.19, s32[]{:T(128)S(6)} %select_n.52, bf16[640]{0:T(1024)(128)(2,1)S(1)} %pad.11.clone, bf16[256,1]{1,0:T(8,128)(2,1)S(1)} %broadcast_in_dim.20, bf16[256,576]{1,0:T(8,128)(2,1)S(1)} %copy.16), kind=kLoop, calls=%fused_computation.21 | loop fusion | flops 983040 | bytes 1050628 | tf_op jit(solution)/shard_map/dynamic_update_slice | solution.py:192
  5.1 2.1 %collective-permute-start = (bf16[256,640]{1,0:T(8,128)(2,1)}, bf16[256,640]{1,0:T(8,128)(2,1)S(1)}, u32[]{:S(2)}, u32[]{:S(2)}) collective-permute-start(bf16[256,640]{1,0:T(8,128)(2,1)} %get-tuple-element.24), channel_id=1, source_target_pairs={{0,2},{2,4},{4,6},{6,7},{7,5},{5,3},{3,1},{1,0},{8,10},{10,12},{12... | collective-permute-start | bytes 983048 | tf_op jit(solution)/shard_map/ppermute | solution.py:181
  7.3 0.0 collective-permute-start.1
  7.3 2.2 %copy.18 = bf16[2048,1,192]{2,0,1:T(8,128)(2,1)} copy(bf16[2048,1,192]{0,2,1:T(8,128)(2,1)} %param.6) | data formatting | bytes 1572864 | tf_op args[0]
  9.5 0.7 %fusion.2 = (s32[8]{0:T(128)}, s32[8]{0:T(128)}) fusion(s32[4,512]{1,0:T(4,128)S(1)} %get-tuple-element.34, s32[4,512]{1,0:T(4,128)S(1)} %get-tuple-element.33), kind=kLoop, calls=%fused_computation.8 | loop fusion | flops 12272 | bytes 16448 | tf_op jit(solution)/shard_map/reduce_max | solution.py:218
  10.2 0.6 broadcast_select_fusion
  10.9 4.0 %collective-permute-done = bf16[256,640]{1,0:T(8,128)(2,1)S(1)} collective-permute-done((bf16[256,640]{1,0:T(8,128)(2,1)}, bf16[256,640]{1,0:T(8,128)(2,1)S(1)}, u32[]{:S(2)}, u32[]{:S(2)}) %collective-permute-start) | collective-permute-done | bytes 327712 | tf_op jit(solution)/shard_map/ppermute | solution.py:181
  14.8 0.9 %collective-permute-done.1 = bf16[256,640]{1,0:T(8,128)(2,1)S(1)} collective-permute-done((bf16[256,640]{1,0:T(8,128)(2,1)}, bf16[256,640]{1,0:T(8,128)(2,1)S(1)}, u32[]{:S(2)}, u32[]{:S(2)}) %collective-permute-start.1) | collective-permute-done | bytes 327712 | tf_op jit(solution)/shard_map/ppermute | solution.py:183
  15.7 1.3 %collective-permute-start.2 = (bf16[256,640]{1,0:T(8,128)(2,1)S(1)}, bf16[256,640]{1,0:T(8,128)(2,1)}, u32[]{:S(2)}, u32[]{:S(2)}) collective-permute-start(bf16[256,640]{1,0:T(8,128)(2,1)S(1)} %collective-permute-done), channel_id=1, source_target_pairs={{0,2},{2,4},{4,6},{6,7},{7,5},{5,3},{3,1},{1,0},{8,10},{10,12},{12... | collective-permute-start | bytes 983048 | tf_op jit(solution)/shard_map/ppermute | solution.py:181
  17.0 0.2 collective-permute-start.3
  21.5 1.6 %collective-permute-done.2 = bf16[256,640]{1,0:T(8,128)(2,1)} collective-permute-done((bf16[256,640]{1,0:T(8,128)(2,1)S(1)}, bf16[256,640]{1,0:T(8,128)(2,1)}, u32[]{:S(2)}, u32[]{:S(2)}) %collective-permute-start.2) | collective-permute-done | bytes 327712 | tf_op jit(solution)/shard_map/ppermute | solution.py:181
  23.2 1.3 %collective-permute-start.4 = (bf16[256,640]{1,0:T(8,128)(2,1)}, bf16[256,640]{1,0:T(8,128)(2,1)S(1)}, u32[]{:S(2)}, u32[]{:S(2)}) collective-permute-start(bf16[256,640]{1,0:T(8,128)(2,1)} %collective-permute-done.2), channel_id=1, source_target_pairs={{0,2},{2,4},{4,6},{6,7},{7,5},{5,3},{3,1},{1,0},{8,10},{10,12},{12... | collective-permute-start | bytes 983048 | tf_op jit(solution)/shard_map/ppermute | solution.py:181
  24.6 0.0 collective-permute-done.3
  24.6 0.2 collective-permute-start.5
  24.8 1.0 %constant_dynamic-update-slice_fusion.4 = bf16[2048,640]{1,0:T(8,128)(2,1)S(1)} fusion(bf16[2048,640]{1,0:T(8,128)(2,1)S(1)} %constant_dynamic-update-slice_fusion.5, bf16[256,640]{1,0:T(8,128)(2,1)} %collective-permute-done.2, s32[]{:T(128)S(6)} %select_n.55), kind=kLoop, calls=%fused_computation.18 | loop fusion | bytes 655364 | tf_op jit(solution)/shard_map/dynamic_update_slice | solution.py:192
  25.8 4.0 %collective-permute-done.4 = bf16[256,640]{1,0:T(8,128)(2,1)S(1)} collective-permute-done((bf16[256,640]{1,0:T(8,128)(2,1)}, bf16[256,640]{1,0:T(8,128)(2,1)S(1)}, u32[]{:S(2)}, u32[]{:S(2)}) %collective-permute-start.4) | collective-permute-done | bytes 327712 | tf_op jit(solution)/shard_map/ppermute | solution.py:181
  29.8 1.3 %collective-permute-start.6 = (bf16[256,640]{1,0:T(8,128)(2,1)S(1)}, bf16[256,640]{1,0:T(8,128)(2,1)S(1)}, u32[]{:S(2)}, u32[]{:S(2)}) collective-permute-start(bf16[256,640]{1,0:T(8,128)(2,1)S(1)} %collective-permute-done.4), channel_id=1, source_target_pairs={{0,2},{2,4},{4,6},{6,7},{7,5},{5,3},{3,1},{1,0},{8,10},{10,12},{12... | collective-permute-start | bytes 983048 | tf_op jit(solution)/shard_map/ppermute | solution.py:181
  31.1 1.0 %constant_dynamic-update-slice_fusion.3 = bf16[2048,640]{1,0:T(8,128)(2,1)S(1)} fusion(bf16[2048,640]{1,0:T(8,128)(2,1)S(1)} %constant_dynamic-update-slice_fusion.4, bf16[256,640]{1,0:T(8,128)(2,1)} %collective-permute-done.3, s32[]{:T(128)S(6)} %select_n.56), kind=kLoop, calls=%fused_computation.17 | loop fusion | bytes 655364 | tf_op jit(solution)/shard_map/dynamic_update_slice | solution.py:192
  32.2 0.0 collective-permute-done.5
  32.2 0.0 copy-start.4
  32.3 4.1 %collective-permute-done.6 = bf16[256,640]{1,0:T(8,128)(2,1)S(1)} collective-permute-done((bf16[256,640]{1,0:T(8,128)(2,1)S(1)}, bf16[256,640]{1,0:T(8,128)(2,1)S(1)}, u32[]{:S(2)}, u32[]{:S(2)}) %collective-permute-start.6) | collective-permute-done | bytes 327712 | tf_op jit(solution)/shard_map/ppermute | solution.py:181
  36.4 0.0 copy-done
  36.4 0.0 copy-start.3
  36.5 0.7 %convolution_convert_fusion = bf16[2048,128]{1,0:T(8,128)(2,1)S(1)} fusion(bf16[512,128]{1,0:T(8,128)(2,1)S(1)} %copy-done, bf16[2048,640]{1,0:T(8,128)(2,1)S(1)} %constant_dynamic-update-slice_fusion), kind=kOutput, calls=%fused_computation | convolution fusion | flops 268697600 | bytes 2752512 | tf_op jit(solution)/shard_map/dot_general | solution.py:228
  37.2 0.0 copy-done.4
  37.2 0.7 %convolution_convert_fusion.1 = bf16[2048,128]{1,0:T(8,128)(2,1)S(1)} fusion(bf16[512,128]{1,0:T(8,128)(2,1)S(1)} %copy-done.4, bf16[2048,640]{1,0:T(8,128)(2,1)S(1)} %constant_dynamic-update-slice_fusion), kind=kOutput, calls=%fused_computation.1 | convolution fusion | flops 268697600 | bytes 2752512 | tf_op jit(solution)/shard_map/dot_general | solution.py:225
  37.9 0.0 copy-done.3
  37.9 0.2 pad_maximum_fusion.rest_4_.rest_5_.rest_6_
  38.1 0.0 copy-start.1
  38.1 1.3 %collective-permute-start.7 = (bf16[2048,384]{1,0:T(8,128)(2,1)S(1)}, bf16[2048,384]{1,0:T(8,128)(2,1)S(1)}, u32[]{:S(2)}, u32[]{:S(2)}) collective-permute-start(bf16[2048,384]{1,0:T(8,128)(2,1)S(1)} %pad_maximum_fusion.rest_4_.rest_5_.rest_6_), channel_id=1, source_target_pairs={{0,8},{1,9},{2,10},{3,11},{4,12},{5,13},{6,14},{7,15},{16,24},{17,... | collective-permute-start | bytes 4718600 | tf_op jit(solution)/shard_map/ppermute | solution.py:243
  39.4 1.1 %slice.63 = bf16[4,1]{1,0:T(4,128)(2,1)S(1)} slice(bf16[2048,128]{1,0:T(8,128)(2,1)} %copy-done.3), slice={[511:2048:512], [64:65:1]} | slice | bytes 16 | tf_op jit(solution)/shard_map/slice | solution.py:237
  40.5 1.1 %slice.61 = bf16[4,1]{1,0:T(4,128)(2,1)S(1)} slice(bf16[2048,128]{1,0:T(8,128)(2,1)} %copy-done.3), slice={[0:2048:512], [64:65:1]} | slice | bytes 16 | tf_op jit(solution)/shard_map/slice | solution.py:236
  41.6 0.1 reduce.3
  41.8 0.1 reduce.1
  41.9 5.2 %collective-permute-done.7.rest_0_.rest_1_.rest_2_ = bf16[2048,384]{1,0:T(8,128)(2,1)S(1)} collective-permute-done((bf16[2048,384]{1,0:T(8,128)(2,1)S(1)}, bf16[2048,384]{1,0:T(8,128)(2,1)S(1)}, u32[]{:S(2)}, u32[]{:S(2)}) %collective-permute-start.7) | collective-permute-done | bytes 1572896 | tf_op jit(solution)/shard_map/ppermute | solution.py:243
  47.1 0.0 copy-start.2
  47.1 0.2 slice.62
  47.3 0.1 reduce.2
  47.4 0.2 slice.60
  47.6 0.1 reduce
  47.7 0.6 maximum_convert_fusion.1.kmaxd_ref
  48.3 0.6 maximum_convert_fusion.kmind_ref
  48.9 0.0 copy-done.1
  48.9 0.0 copy-done.2
  48.9 18.0 %shard_map.64 = bf16[2048,128]{1,0:T(8,128)(2,1)} custom-call(s32[1]{0:T(128)} %bitcast.qbase_ref, s32[8]{0:T(128)} %get-tuple-element.14.kminp_ref, s32[8]{0:T(128)} %get-tuple-element.15.kmaxp_ref, s32[8]{0:T(128)} %maximum_convert_fusion.kmind_ref, s32[8]{0:T(128)} %maximum_convert_fusion.1.kmaxd_ref, bf16[1,2048,192]{2,1,0:T(8,128)(2,1)} %bitcast.12, ...), custom_call_target="tpu_custom_call" | custom-call | tf_op jit(solution)/shard_map/pallas_call | solution.py:142
  (8 shorter events, 0.3 us)
Async XLA Ops:
  0.0 36.4 %copy-start = (bf16[512,128]{1,0:T(8,128)(2,1)S(1)}, bf16[512,128]{1,0:T(8,128)(2,1)}, u32[]{:S(2)}) copy-start(bf16[512,128]{1,0:T(8,128)(2,1)} %param.10) | copy-start | bytes 393220
  5.1 9.7 %collective-permute-start = (bf16[256,640]{1,0:T(8,128)(2,1)}, bf16[256,640]{1,0:T(8,128)(2,1)S(1)}, u32[]{:S(2)}, u32[]{:S(2)}) collective-permute-start(bf16[256,640]{1,0:T(8,128)(2,1)} %get-tuple-element.24), channel_id=1, source_target_pairs={{0,2},{2,4},{4,6},{6,7},{7,5},{5,3},{3,1},{1,0},{8,10},{10,12},{12... | collective-permute-start | bytes 983048 | tf_op jit(solution)/shard_map/ppermute | solution.py:181
  7.3 8.5 %collective-permute-start.1 = (bf16[256,640]{1,0:T(8,128)(2,1)}, bf16[256,640]{1,0:T(8,128)(2,1)S(1)}, u32[]{:S(2)}, u32[]{:S(2)}) collective-permute-start(bf16[256,640]{1,0:T(8,128)(2,1)} %get-tuple-element.24), channel_id=1, source_target_pairs={{2,0},{4,2},{6,4},{7,6},{5,7},{3,5},{1,3},{0,1},{10,8},{12,10},{14... | collective-permute-start | bytes 983048 | tf_op jit(solution)/shard_map/ppermute | solution.py:183
  15.7 7.4 %collective-permute-start.2 = (bf16[256,640]{1,0:T(8,128)(2,1)S(1)}, bf16[256,640]{1,0:T(8,128)(2,1)}, u32[]{:S(2)}, u32[]{:S(2)}) collective-permute-start(bf16[256,640]{1,0:T(8,128)(2,1)S(1)} %collective-permute-done), channel_id=1, source_target_pairs={{0,2},{2,4},{4,6},{6,7},{7,5},{5,3},{3,1},{1,0},{8,10},{10,12},{12... | collective-permute-start | bytes 983048 | tf_op jit(solution)/shard_map/ppermute | solution.py:181
  17.0 7.5 %collective-permute-start.3 = (bf16[256,640]{1,0:T(8,128)(2,1)S(1)}, bf16[256,640]{1,0:T(8,128)(2,1)}, u32[]{:S(2)}, u32[]{:S(2)}) collective-permute-start(bf16[256,640]{1,0:T(8,128)(2,1)S(1)} %collective-permute-done.1), channel_id=1, source_target_pairs={{2,0},{4,2},{6,4},{7,6},{5,7},{3,5},{1,3},{0,1},{10,8},{12,10},{14... | collective-permute-start | bytes 983048 | tf_op jit(solution)/shard_map/ppermute | solution.py:183
  23.2 6.6 %collective-permute-start.4 = (bf16[256,640]{1,0:T(8,128)(2,1)}, bf16[256,640]{1,0:T(8,128)(2,1)S(1)}, u32[]{:S(2)}, u32[]{:S(2)}) collective-permute-start(bf16[256,640]{1,0:T(8,128)(2,1)} %collective-permute-done.2), channel_id=1, source_target_pairs={{0,2},{2,4},{4,6},{6,7},{7,5},{5,3},{3,1},{1,0},{8,10},{10,12},{12... | collective-permute-start | bytes 983048 | tf_op jit(solution)/shard_map/ppermute | solution.py:181
  24.6 7.6 %collective-permute-start.5 = (bf16[256,640]{1,0:T(8,128)(2,1)}, bf16[256,640]{1,0:T(8,128)(2,1)S(1)}, u32[]{:S(2)}, u32[]{:S(2)}) collective-permute-start(bf16[256,640]{1,0:T(8,128)(2,1)} %collective-permute-done.3), channel_id=1, source_target_pairs={{2,0},{4,2},{6,4},{7,6},{5,7},{3,5},{1,3},{0,1},{10,8},{12,10},{14... | collective-permute-start | bytes 983048 | tf_op jit(solution)/shard_map/ppermute | solution.py:183
  29.8 6.5 %collective-permute-start.6 = (bf16[256,640]{1,0:T(8,128)(2,1)S(1)}, bf16[256,640]{1,0:T(8,128)(2,1)S(1)}, u32[]{:S(2)}, u32[]{:S(2)}) collective-permute-start(bf16[256,640]{1,0:T(8,128)(2,1)S(1)} %collective-permute-done.4), channel_id=1, source_target_pairs={{0,2},{2,4},{4,6},{6,7},{7,5},{5,3},{3,1},{1,0},{8,10},{10,12},{12... | collective-permute-start | bytes 983048 | tf_op jit(solution)/shard_map/ppermute | solution.py:181
  32.2 4.9 %copy-start.4 = (bf16[512,128]{1,0:T(8,128)(2,1)S(1)}, bf16[512,128]{1,0:T(8,128)(2,1)}, u32[]{:S(2)}) copy-start(bf16[512,128]{1,0:T(8,128)(2,1)} %param.9) | copy-start | bytes 393220
  36.4 1.4 %copy-start.3 = (bf16[2048,128]{1,0:T(8,128)(2,1)}, bf16[2048,128]{1,0:T(8,128)(2,1)S(1)}, u32[]{:S(2)}) copy-start(bf16[2048,128]{1,0:T(8,128)(2,1)S(1)} %slice.65) | copy-start | bytes 1572868
  38.1 10.8 %copy-start.1 = (bf16[2048,384]{1,0:T(8,128)(2,1)}, bf16[2048,384]{1,0:T(8,128)(2,1)S(1)}, u32[]{:S(2)}) copy-start(bf16[2048,384]{1,0:T(8,128)(2,1)S(1)} %pad_maximum_fusion.rest_4_.rest_5_.rest_6_) | copy-start | bytes 4718596
  38.1 9.0 %collective-permute-start.7 = (bf16[2048,384]{1,0:T(8,128)(2,1)S(1)}, bf16[2048,384]{1,0:T(8,128)(2,1)S(1)}, u32[]{:S(2)}, u32[]{:S(2)}) collective-permute-start(bf16[2048,384]{1,0:T(8,128)(2,1)S(1)} %pad_maximum_fusion.rest_4_.rest_5_.rest_6_), channel_id=1, source_target_pairs={{0,8},{1,9},{2,10},{3,11},{4,12},{5,13},{6,14},{7,15},{16,24},{17,... | collective-permute-start | bytes 4718600 | tf_op jit(solution)/shard_map/ppermute | solution.py:243
  47.1 1.8 %copy-start.2 = (bf16[2048,384]{1,0:T(8,128)(2,1)}, bf16[2048,384]{1,0:T(8,128)(2,1)S(1)}, u32[]{:S(2)}) copy-start(bf16[2048,384]{1,0:T(8,128)(2,1)S(1)} %collective-permute-done.7.rest_0_.rest_1_.rest_2_) | copy-start | bytes 4718596
where the time goes:
time: 67.3 us; the launch traced here: 66.9 us
  waiting for transfers between devices  19.8 us (29%)
  Pallas kernels  18 us (27%)
  local copies, waits for them, and re-layouts  10 us (15%)
  starting transfers between devices  7.7 us (11%)
  between operations  5.17 us (8%)
  other arithmetic  4.79 us (7%)
  matrix products  1.41 us (2%)
    pallas_call x1, Pallas kernels, flash(): pl.pallas_call(kernel, grid_spec=grid_spec, out_shape=jax.ShapeDtypeStruc...  18 us
    ppermute x4, waiting for transfers between devices, ring_gather(): moving_f = lax.ppermute(moving_f, 'tp', forward)  13.7 us
    ppermute x4, starting transfers between devices, ring_gather(): moving_f = lax.ppermute(moving_f, 'tp', forward)  6.01 us
    ppermute x1, waiting for transfers between devices, body(): moved = lax.ppermute(pack, 'ctx', route)  5.21 us
    unnamed x12, local copies, waits for them, and re-layouts  3.42 us
    dynamic_update_slice x7, local copies, waits for them, and re-layouts, ring_gather(): lax.dynamic_update_slice(placed, piece, (source_of[number] * rows, 0))  2.24 us
  transfers between devices with their start and end apart: 8, of which 6 were waited for; matrix products, arithmetic and copies ran while one was open for 12% of the time, Pallas kernels for 0%

commit v1 on v0

--- a/solution.py
+++ b/solution.py
@@ -39,7 +39,17 @@
     q_doc = set_refs[-1][2][pl.ds(pl.multiple_of(qt * bq, bq), bq), :][:, ROPE_DIM : ROPE_DIM + 1].astype(jnp.float32)
     nt = (((1,), (1,)), ((), ()))
 
-    m_sc, l_sc, acc_sc = rest[4 * sets + 1 :]
+    m_sc, l_sc, acc_sc, kdoc_sc = rest[4 * sets + 1 :]
+
+    @pl.when(qt == 0)
+    def _():
+        for number, refs in enumerate(set_refs):
+            for t in range(tiles):
+                block = refs[2][t * bk : (t + 1) * bk, :].astype(jnp.float32)
+                kdoc_sc[number * 8 : number * 8 + 1, t * bk : (t + 1) * bk] = jnp.transpose(
+                    block
+                )[ROPE_DIM : ROPE_DIM + 1, :]
+
     m_sc[...] = jnp.full(m_sc.shape, -1e30, jnp.float32)
     l_sc[...] = jnp.zeros(l_sc.shape, jnp.float32)
     acc_sc[...] = jnp.zeros(acc_sc.shape, jnp.float32)
@@ -56,7 +66,7 @@
             scores = scores * factor
             if masked:
                 k_pos = kp_ref[:, pl.ds(start, bk)]
-                k_doc = jnp.transpose(ropes.astype(jnp.float32))[ROPE_DIM : ROPE_DIM + 1, :]
+                k_doc = kdoc_sc[pl.ds(number * 8, 1), pl.ds(start, bk)]
                 visible = (k_pos <= q_pos) & (k_doc == q_doc)
                 scores = jnp.where(visible, scores, jnp.float32(-1e30))
             m_prev = m_sc[...]
@@ -137,6 +147,7 @@
             pltpu.VMEM((bq, 1), jnp.float32),
             pltpu.VMEM((bq, 1), jnp.float32),
             pltpu.VMEM((bq, LANES), jnp.float32),
+            pltpu.VMEM((8 * sets, count), jnp.float32),
         ],
     )
     return pl.pallas_call(

time: 67.3 us -> 69.6 us (1.034)
  the two profiles are of different devices: /device:TPU:1 before, /device:TPU:21 now
where the time goes in v1:
time: 69.6 us; the launch traced here: 69.1 us
  Pallas kernels  21 us (30%)
  waiting for transfers between devices  19.7 us (28%)
  local copies, waits for them, and re-layouts  10 us (14%)
  starting transfers between devices  6.95 us (10%)
  between operations  5.17 us (7%)
  other arithmetic  4.79 us (7%)
  matrix products  1.41 us (2%)
    pallas_call x1, Pallas kernels, flash(): pl.pallas_call(kernel, grid_spec=grid_spec, out_shape=jax.ShapeDtypeStruc...  21 us
    ppermute x4, waiting for transfers between devices, ring_gather(): moving_f = lax.ppermute(moving_f, 'tp', forward)  13.5 us
    ppermute x1, waiting for transfers between devices, body(): moved = lax.ppermute(pack, 'ctx', route)  5.21 us
    ppermute x4, starting transfers between devices, ring_gather(): moving_f = lax.ppermute(moving_f, 'tp', forward)  4.93 us
    unnamed x12, local copies, waits for them, and re-layouts  3.42 us
    dynamic_update_slice x7, local copies, waits for them, and re-layouts, ring_gather(): lax.dynamic_update_slice(placed, piece, (source_of[number] * rows, 0))  2.24 us
  transfers between devices with their start and end apart: 8, of which 6 were waited for; matrix products, arithmetic and copies ran while one was open for 12% of the time, Pallas kernels for 0%

profile of v1, /device:TPU:21, one launch (start us, length us, event | category | flops | bytes accessed | tf_op | source)
XLA Modules:
  0.0 69.1 jit_solution(16198023834655715702)
XLA Ops:
  0.0 0.0 copy-start
  0.0 0.7 %constant_dynamic-slice_fusion = s32[1,8]{1,0:T(1,128)S(1)} fusion(s32[8,8]{1,0:T(8,128)} %constant.42.clone, s32[]{:T(128)S(6)} %select_n.51), kind=kLoop, calls=%fused_computation.22 | loop fusion | bytes 68 | tf_op jit(solution)/shard_map/dynamic_slice | solution.py:178
  0.7 0.7 fusion.5
  2.0 1.2 %copy.16 = bf16[256,576]{1,0:T(8,128)(2,1)S(1)} copy(bf16[256,576]{0,1:T(8,128)(2,1)} %param.7) | data formatting | bytes 589824 | tf_op args[1]
  3.2 0.7 convert_element_type.25
  3.9 0.1 broadcast_in_dim.20
  4.0 0.1 pad.11.clone
  4.1 0.2 broadcast_in_dim.19
  4.3 0.8 %constant_dynamic-update-slice_fusion.7 = (bf16[2048,640]{1,0:T(8,128)(2,1)S(1)}, bf16[256,640]{1,0:T(8,128)(2,1)}) fusion(bf16[2048,640]{1,0:T(8,128)(2,1)S(1)} %broadcast_in_dim.19, s32[]{:T(128)S(6)} %select_n.52, bf16[640]{0:T(1024)(128)(2,1)S(1)} %pad.11.clone, bf16[256,1]{1,0:T(8,128)(2,1)S(1)} %broadcast_in_dim.20, bf16[256,576]{1,0:T(8,128)(2,1)S(1)} %copy.16), kind=kLoop, calls=%fused_computation.21 | loop fusion | flops 983040 | bytes 1050628 | tf_op jit(solution)/shard_map/dynamic_update_slice | solution.py:203
  5.1 1.3 %collective-permute-start = (bf16[256,640]{1,0:T(8,128)(2,1)}, bf16[256,640]{1,0:T(8,128)(2,1)S(1)}, u32[]{:S(2)}, u32[]{:S(2)}) collective-permute-start(bf16[256,640]{1,0:T(8,128)(2,1)} %get-tuple-element.24), channel_id=1, source_target_pairs={{0,2},{2,4},{4,6},{6,7},{7,5},{5,3},{3,1},{1,0},{8,10},{10,12},{12... | collective-permute-start | bytes 983048 | tf_op jit(solution)/shard_map/ppermute | solution.py:192
  6.4 0.2 collective-permute-start.1
  6.6 2.2 %copy.18 = bf16[2048,1,192]{2,0,1:T(8,128)(2,1)} copy(bf16[2048,1,192]{0,2,1:T(8,128)(2,1)} %param.6) | data formatting | bytes 1572864 | tf_op args[0]
  8.8 0.7 %fusion.2 = (s32[8]{0:T(128)}, s32[8]{0:T(128)}) fusion(s32[4,512]{1,0:T(4,128)S(1)} %get-tuple-element.34, s32[4,512]{1,0:T(4,128)S(1)} %get-tuple-element.33), kind=kLoop, calls=%fused_computation.8 | loop fusion | flops 12272 | bytes 16448 | tf_op jit(solution)/shard_map/reduce_max | solution.py:229
  9.6 0.6 broadcast_select_fusion
  10.2 3.7 %collective-permute-done = bf16[256,640]{1,0:T(8,128)(2,1)S(1)} collective-permute-done((bf16[256,640]{1,0:T(8,128)(2,1)}, bf16[256,640]{1,0:T(8,128)(2,1)S(1)}, u32[]{:S(2)}, u32[]{:S(2)}) %collective-permute-start) | collective-permute-done | bytes 327712 | tf_op jit(solution)/shard_map/ppermute | solution.py:192
  13.9 1.0 %collective-permute-done.1 = bf16[256,640]{1,0:T(8,128)(2,1)S(1)} collective-permute-done((bf16[256,640]{1,0:T(8,128)(2,1)}, bf16[256,640]{1,0:T(8,128)(2,1)S(1)}, u32[]{:S(2)}, u32[]{:S(2)}) %collective-permute-start.1) | collective-permute-done | bytes 327712 | tf_op jit(solution)/shard_map/ppermute | solution.py:194
  14.9 1.2 %collective-permute-start.2 = (bf16[256,640]{1,0:T(8,128)(2,1)S(1)}, bf16[256,640]{1,0:T(8,128)(2,1)}, u32[]{:S(2)}, u32[]{:S(2)}) collective-permute-start(bf16[256,640]{1,0:T(8,128)(2,1)S(1)} %collective-permute-done), channel_id=1, source_target_pairs={{0,2},{2,4},{4,6},{6,7},{7,5},{5,3},{3,1},{1,0},{8,10},{10,12},{12... | collective-permute-start | bytes 983048 | tf_op jit(solution)/shard_map/ppermute | solution.py:192
  16.1 0.3 collective-permute-start.3
  20.7 1.6 %collective-permute-done.2 = bf16[256,640]{1,0:T(8,128)(2,1)} collective-permute-done((bf16[256,640]{1,0:T(8,128)(2,1)S(1)}, bf16[256,640]{1,0:T(8,128)(2,1)}, u32[]{:S(2)}, u32[]{:S(2)}) %collective-permute-start.2) | collective-permute-done | bytes 327712 | tf_op jit(solution)/shard_map/ppermute | solution.py:192
  22.4 1.2 %collective-permute-start.4 = (bf16[256,640]{1,0:T(8,128)(2,1)}, bf16[256,640]{1,0:T(8,128)(2,1)S(1)}, u32[]{:S(2)}, u32[]{:S(2)}) collective-permute-start(bf16[256,640]{1,0:T(8,128)(2,1)} %collective-permute-done.2), channel_id=1, source_target_pairs={{0,2},{2,4},{4,6},{6,7},{7,5},{5,3},{3,1},{1,0},{8,10},{10,12},{12... | collective-permute-start | bytes 983048 | tf_op jit(solution)/shard_map/ppermute | solution.py:192
  23.7 0.0 collective-permute-done.3
  23.7 0.3 collective-permute-start.5
  24.0 1.0 %constant_dynamic-update-slice_fusion.4 = bf16[2048,640]{1,0:T(8,128)(2,1)S(1)} fusion(bf16[2048,640]{1,0:T(8,128)(2,1)S(1)} %constant_dynamic-update-slice_fusion.5, bf16[256,640]{1,0:T(8,128)(2,1)} %collective-permute-done.2, s32[]{:T(128)S(6)} %select_n.55), kind=kLoop, calls=%fused_computation.18 | loop fusion | bytes 655364 | tf_op jit(solution)/shard_map/dynamic_update_slice | solution.py:203
  25.0 4.0 %collective-permute-done.4 = bf16[256,640]{1,0:T(8,128)(2,1)S(1)} collective-permute-done((bf16[256,640]{1,0:T(8,128)(2,1)}, bf16[256,640]{1,0:T(8,128)(2,1)S(1)}, u32[]{:S(2)}, u32[]{:S(2)}) %collective-permute-start.4) | collective-permute-done | bytes 327712 | tf_op jit(solution)/shard_map/ppermute | solution.py:192
  29.0 1.2 %collective-permute-start.6 = (bf16[256,640]{1,0:T(8,128)(2,1)S(1)}, bf16[256,640]{1,0:T(8,128)(2,1)S(1)}, u32[]{:S(2)}, u32[]{:S(2)}) collective-permute-start(bf16[256,640]{1,0:T(8,128)(2,1)S(1)} %collective-permute-done.4), channel_id=1, source_target_pairs={{0,2},{2,4},{4,6},{6,7},{7,5},{5,3},{3,1},{1,0},{8,10},{10,12},{12... | collective-permute-start | bytes 983048 | tf_op jit(solution)/shard_map/ppermute | solution.py:192
  30.2 1.0 %constant_dynamic-update-slice_fusion.3 = bf16[2048,640]{1,0:T(8,128)(2,1)S(1)} fusion(bf16[2048,640]{1,0:T(8,128)(2,1)S(1)} %constant_dynamic-update-slice_fusion.4, bf16[256,640]{1,0:T(8,128)(2,1)} %collective-permute-done.3, s32[]{:T(128)S(6)} %select_n.56), kind=kLoop, calls=%fused_computation.17 | loop fusion | bytes 655364 | tf_op jit(solution)/shard_map/dynamic_update_slice | solution.py:203
  31.3 0.0 collective-permute-done.5
  31.3 0.0 copy-start.4
  31.3 4.2 %collective-permute-done.6 = bf16[256,640]{1,0:T(8,128)(2,1)S(1)} collective-permute-done((bf16[256,640]{1,0:T(8,128)(2,1)S(1)}, bf16[256,640]{1,0:T(8,128)(2,1)S(1)}, u32[]{:S(2)}, u32[]{:S(2)}) %collective-permute-start.6) | collective-permute-done | bytes 327712 | tf_op jit(solution)/shard_map/ppermute | solution.py:192
  35.6 0.0 copy-done
  35.6 0.0 copy-start.3
  35.6 0.7 %convolution_convert_fusion = bf16[2048,128]{1,0:T(8,128)(2,1)S(1)} fusion(bf16[512,128]{1,0:T(8,128)(2,1)S(1)} %copy-done, bf16[2048,640]{1,0:T(8,128)(2,1)S(1)} %constant_dynamic-update-slice_fusion), kind=kOutput, calls=%fused_computation | convolution fusion | flops 268697600 | bytes 2752512 | tf_op jit(solution)/shard_map/dot_general | solution.py:239
  36.3 0.0 copy-done.4
  36.3 0.7 %convolution_convert_fusion.1 = bf16[2048,128]{1,0:T(8,128)(2,1)S(1)} fusion(bf16[512,128]{1,0:T(8,128)(2,1)S(1)} %copy-done.4, bf16[2048,640]{1,0:T(8,128)(2,1)S(1)} %constant_dynamic-update-slice_fusion), kind=kOutput, calls=%fused_computation.1 | convolution fusion | flops 268697600 | bytes 2752512 | tf_op jit(solution)/shard_map/dot_general | solution.py:236
  37.1 0.0 copy-done.3
  37.1 0.2 pad_maximum_fusion.rest_4_.rest_5_.rest_6_
  37.3 0.0 copy-start.1
  37.3 1.3 %collective-permute-start.7 = (bf16[2048,384]{1,0:T(8,128)(2,1)S(1)}, bf16[2048,384]{1,0:T(8,128)(2,1)S(1)}, u32[]{:S(2)}, u32[]{:S(2)}) collective-permute-start(bf16[2048,384]{1,0:T(8,128)(2,1)S(1)} %pad_maximum_fusion.rest_4_.rest_5_.rest_6_), channel_id=1, source_target_pairs={{0,8},{1,9},{2,10},{3,11},{4,12},{5,13},{6,14},{7,15},{16,24},{17,... | collective-permute-start | bytes 4718600 | tf_op jit(solution)/shard_map/ppermute | solution.py:254
  38.6 1.1 %slice.63 = bf16[4,1]{1,0:T(4,128)(2,1)S(1)} slice(bf16[2048,128]{1,0:T(8,128)(2,1)} %copy-done.3), slice={[511:2048:512], [64:65:1]} | slice | bytes 16 | tf_op jit(solution)/shard_map/slice | solution.py:248
  39.7 1.1 %slice.61 = bf16[4,1]{1,0:T(4,128)(2,1)S(1)} slice(bf16[2048,128]{1,0:T(8,128)(2,1)} %copy-done.3), slice={[0:2048:512], [64:65:1]} | slice | bytes 16 | tf_op jit(solution)/shard_map/slice | solution.py:247
  40.8 0.1 reduce.3
  40.9 0.1 reduce.1
  41.1 5.2 %collective-permute-done.7.rest_0_.rest_1_.rest_2_ = bf16[2048,384]{1,0:T(8,128)(2,1)S(1)} collective-permute-done((bf16[2048,384]{1,0:T(8,128)(2,1)S(1)}, bf16[2048,384]{1,0:T(8,128)(2,1)S(1)}, u32[]{:S(2)}, u32[]{:S(2)}) %collective-permute-start.7) | collective-permute-done | bytes 1572896 | tf_op jit(solution)/shard_map/ppermute | solution.py:254
  46.3 0.0 copy-start.2
  46.3 0.2 slice.62
  46.4 0.1 reduce.2
  46.5 0.2 slice.60
  46.7 0.1 reduce
  46.9 0.6 maximum_convert_fusion.1.kmaxd_ref
  47.4 0.6 maximum_convert_fusion.kmind_ref
  48.1 0.0 copy-done.1
  48.1 0.0 copy-done.2
  48.1 21.0 %shard_map.64 = bf16[2048,128]{1,0:T(8,128)(2,1)} custom-call(s32[1]{0:T(128)} %bitcast.qbase_ref, s32[8]{0:T(128)} %get-tuple-element.14.kminp_ref, s32[8]{0:T(128)} %get-tuple-element.15.kmaxp_ref, s32[8]{0:T(128)} %maximum_convert_fusion.kmind_ref, s32[8]{0:T(128)} %maximum_convert_fusion.1.kmaxd_ref, bf16[1,2048,192]{2,1,0:T(8,128)(2,1)} %bitcast.12, ...), custom_call_target="tpu_custom_call" | custom-call | tf_op jit(solution)/shard_map/pallas_call | solution.py:153
  (8 shorter events, 0.3 us)
Async XLA Ops:
  0.0 35.6 %copy-start = (bf16[512,128]{1,0:T(8,128)(2,1)S(1)}, bf16[512,128]{1,0:T(8,128)(2,1)}, u32[]{:S(2)}) copy-start(bf16[512,128]{1,0:T(8,128)(2,1)} %param.10) | copy-start | bytes 393220
  5.1 8.8 %collective-permute-start = (bf16[256,640]{1,0:T(8,128)(2,1)}, bf16[256,640]{1,0:T(8,128)(2,1)S(1)}, u32[]{:S(2)}, u32[]{:S(2)}) collective-permute-start(bf16[256,640]{1,0:T(8,128)(2,1)} %get-tuple-element.24), channel_id=1, source_target_pairs={{0,2},{2,4},{4,6},{6,7},{7,5},{5,3},{3,1},{1,0},{8,10},{10,12},{12... | collective-permute-start | bytes 983048 | tf_op jit(solution)/shard_map/ppermute | solution.py:192
  6.4 8.5 %collective-permute-start.1 = (bf16[256,640]{1,0:T(8,128)(2,1)}, bf16[256,640]{1,0:T(8,128)(2,1)S(1)}, u32[]{:S(2)}, u32[]{:S(2)}) collective-permute-start(bf16[256,640]{1,0:T(8,128)(2,1)} %get-tuple-element.24), channel_id=1, source_target_pairs={{2,0},{4,2},{6,4},{7,6},{5,7},{3,5},{1,3},{0,1},{10,8},{12,10},{14... | collective-permute-start | bytes 983048 | tf_op jit(solution)/shard_map/ppermute | solution.py:194
  14.9 7.4 %collective-permute-start.2 = (bf16[256,640]{1,0:T(8,128)(2,1)S(1)}, bf16[256,640]{1,0:T(8,128)(2,1)}, u32[]{:S(2)}, u32[]{:S(2)}) collective-permute-start(bf16[256,640]{1,0:T(8,128)(2,1)S(1)} %collective-permute-done), channel_id=1, source_target_pairs={{0,2},{2,4},{4,6},{6,7},{7,5},{5,3},{3,1},{1,0},{8,10},{10,12},{12... | collective-permute-start | bytes 983048 | tf_op jit(solution)/shard_map/ppermute | solution.py:192
  16.1 7.5 %collective-permute-start.3 = (bf16[256,640]{1,0:T(8,128)(2,1)S(1)}, bf16[256,640]{1,0:T(8,128)(2,1)}, u32[]{:S(2)}, u32[]{:S(2)}) collective-permute-start(bf16[256,640]{1,0:T(8,128)(2,1)S(1)} %collective-permute-done.1), channel_id=1, source_target_pairs={{2,0},{4,2},{6,4},{7,6},{5,7},{3,5},{1,3},{0,1},{10,8},{12,10},{14... | collective-permute-start | bytes 983048 | tf_op jit(solution)/shard_map/ppermute | solution.py:194
  22.4 6.6 %collective-permute-start.4 = (bf16[256,640]{1,0:T(8,128)(2,1)}, bf16[256,640]{1,0:T(8,128)(2,1)S(1)}, u32[]{:S(2)}, u32[]{:S(2)}) collective-permute-start(bf16[256,640]{1,0:T(8,128)(2,1)} %collective-permute-done.2), channel_id=1, source_target_pairs={{0,2},{2,4},{4,6},{6,7},{7,5},{5,3},{3,1},{1,0},{8,10},{10,12},{12... | collective-permute-start | bytes 983048 | tf_op jit(solution)/shard_map/ppermute | solution.py:192
  23.7 7.6 %collective-permute-start.5 = (bf16[256,640]{1,0:T(8,128)(2,1)}, bf16[256,640]{1,0:T(8,128)(2,1)S(1)}, u32[]{:S(2)}, u32[]{:S(2)}) collective-permute-start(bf16[256,640]{1,0:T(8,128)(2,1)} %collective-permute-done.3), channel_id=1, source_target_pairs={{2,0},{4,2},{6,4},{7,6},{5,7},{3,5},{1,3},{0,1},{10,8},{12,10},{14... | collective-permute-start | bytes 983048 | tf_op jit(solution)/shard_map/ppermute | solution.py:194
  29.0 6.5 %collective-permute-start.6 = (bf16[256,640]{1,0:T(8,128)(2,1)S(1)}, bf16[256,640]{1,0:T(8,128)(2,1)S(1)}, u32[]{:S(2)}, u32[]{:S(2)}) collective-permute-start(bf16[256,640]{1,0:T(8,128)(2,1)S(1)} %collective-permute-done.4), channel_id=1, source_target_pairs={{0,2},{2,4},{4,6},{6,7},{7,5},{5,3},{3,1},{1,0},{8,10},{10,12},{12... | collective-permute-start | bytes 983048 | tf_op jit(solution)/shard_map/ppermute | solution.py:192
  31.3 5.0 %copy-start.4 = (bf16[512,128]{1,0:T(8,128)(2,1)S(1)}, bf16[512,128]{1,0:T(8,128)(2,1)}, u32[]{:S(2)}) copy-start(bf16[512,128]{1,0:T(8,128)(2,1)} %param.9) | copy-start | bytes 393220
  35.6 1.4 %copy-start.3 = (bf16[2048,128]{1,0:T(8,128)(2,1)}, bf16[2048,128]{1,0:T(8,128)(2,1)S(1)}, u32[]{:S(2)}) copy-start(bf16[2048,128]{1,0:T(8,128)(2,1)S(1)} %slice.65) | copy-start | bytes 1572868
  37.3 10.8 %copy-start.1 = (bf16[2048,384]{1,0:T(8,128)(2,1)}, bf16[2048,384]{1,0:T(8,128)(2,1)S(1)}, u32[]{:S(2)}) copy-start(bf16[2048,384]{1,0:T(8,128)(2,1)S(1)} %pad_maximum_fusion.rest_4_.rest_5_.rest_6_) | copy-start | bytes 4718596
  37.3 9.0 %collective-permute-start.7 = (bf16[2048,384]{1,0:T(8,128)(2,1)S(1)}, bf16[2048,384]{1,0:T(8,128)(2,1)S(1)}, u32[]{:S(2)}, u32[]{:S(2)}) collective-permute-start(bf16[2048,384]{1,0:T(8,128)(2,1)S(1)} %pad_maximum_fusion.rest_4_.rest_5_.rest_6_), channel_id=1, source_target_pairs={{0,8},{1,9},{2,10},{3,11},{4,12},{5,13},{6,14},{7,15},{16,24},{17,... | collective-permute-start | bytes 4718600 | tf_op jit(solution)/shard_map/ppermute | solution.py:254
  46.3 1.8 %copy-start.2 = (bf16[2048,384]{1,0:T(8,128)(2,1)}, bf16[2048,384]{1,0:T(8,128)(2,1)S(1)}, u32[]{:S(2)}) copy-start(bf16[2048,384]{1,0:T(8,128)(2,1)S(1)} %collective-permute-done.7.rest_0_.rest_1_.rest_2_) | copy-start | bytes 4718596

commit v2 on v0

--- a/solution.py
+++ b/solution.py
@@ -56,7 +56,7 @@
             scores = scores * factor
             if masked:
                 k_pos = kp_ref[:, pl.ds(start, bk)]
-                k_doc = jnp.transpose(ropes.astype(jnp.float32))[ROPE_DIM : ROPE_DIM + 1, :]
+                k_doc = jnp.transpose(ropes)[ROPE_DIM : ROPE_DIM + 1, :].astype(jnp.float32)
                 visible = (k_pos <= q_pos) & (k_doc == q_doc)
                 scores = jnp.where(visible, scores, jnp.float32(-1e30))
             m_prev = m_sc[...]

time: 67.3 us -> 68.9 us (1.024)
  Pallas kernels: 18 us -> 19.6 us
    pallas_call x1, Pallas kernels: 18 us -> 19.6 us  [flash(): pl.pallas_call(kernel, grid_spec=grid_spec, out_shape=jax.ShapeDtypeStruc...]
where the time goes in v2:
time: 68.9 us; the launch traced here: 68.5 us
  waiting for transfers between devices  19.8 us (29%)
  Pallas kernels  19.6 us (28%)
  local copies, waits for them, and re-layouts  10 us (15%)
  starting transfers between devices  7.7 us (11%)
  between operations  5.17 us (8%)
  other arithmetic  4.79 us (7%)
  matrix products  1.41 us (2%)
    pallas_call x1, Pallas kernels, flash(): pl.pallas_call(kernel, grid_spec=grid_spec, out_shape=jax.ShapeDtypeStruc...  19.6 us
    ppermute x4, waiting for transfers between devices, ring_gather(): moving_f = lax.ppermute(moving_f, 'tp', forward)  13.7 us
    ppermute x4, starting transfers between devices, ring_gather(): moving_f = lax.ppermute(moving_f, 'tp', forward)  6.01 us
    ppermute x1, waiting for transfers between devices, body(): moved = lax.ppermute(pack, 'ctx', route)  5.21 us
    unnamed x12, local copies, waits for them, and re-layouts  3.42 us
    dynamic_update_slice x7, local copies, waits for them, and re-layouts, ring_gather(): lax.dynamic_update_slice(placed, piece, (source_of[number] * rows, 0))  2.24 us
  transfers between devices with their start and end apart: 8, of which 6 were waited for; matrix products, arithmetic and copies ran while one was open for 12% of the time, Pallas kernels for 0%

profile of v2, /device:TPU:1, one launch (start us, length us, event | category | flops | bytes accessed | tf_op | source)
XLA Modules:
  0.0 68.5 jit_solution(17889334708804670916)
XLA Ops:
  0.0 0.0 copy-start
  0.0 0.7 %constant_dynamic-slice_fusion = s32[1,8]{1,0:T(1,128)S(1)} fusion(s32[8,8]{1,0:T(8,128)} %constant.42.clone, s32[]{:T(128)S(6)} %select_n.51), kind=kLoop, calls=%fused_computation.22 | loop fusion | bytes 68 | tf_op jit(solution)/shard_map/dynamic_slice | solution.py:167
  0.7 0.7 fusion.5
  2.0 1.2 %copy.16 = bf16[256,576]{1,0:T(8,128)(2,1)S(1)} copy(bf16[256,576]{0,1:T(8,128)(2,1)} %param.7) | data formatting | bytes 589824 | tf_op args[1]
  3.2 0.7 %convert_element_type.25 = bf16[256]{0:T(256)(128)(2,1)S(1)} convert(s32[256]{0:T(256)} %param.8) | non-fusion elementwise | flops 256 | bytes 1536 | tf_op jit(solution)/shard_map/convert_element_type | solution.py:206
  3.9 0.1 broadcast_in_dim.20
  4.0 0.1 pad.11.clone
  4.1 0.2 broadcast_in_dim.19
  4.3 0.8 %constant_dynamic-update-slice_fusion.7 = (bf16[2048,640]{1,0:T(8,128)(2,1)S(1)}, bf16[256,640]{1,0:T(8,128)(2,1)}) fusion(bf16[2048,640]{1,0:T(8,128)(2,1)S(1)} %broadcast_in_dim.19, s32[]{:T(128)S(6)} %select_n.52, bf16[640]{0:T(1024)(128)(2,1)S(1)} %pad.11.clone, bf16[256,1]{1,0:T(8,128)(2,1)S(1)} %broadcast_in_dim.20, bf16[256,576]{1,0:T(8,128)(2,1)S(1)} %copy.16), kind=kLoop, calls=%fused_computation.21 | loop fusion | flops 983040 | bytes 1050628 | tf_op jit(solution)/shard_map/dynamic_update_slice | solution.py:192
  5.1 2.1 %collective-permute-start = (bf16[256,640]{1,0:T(8,128)(2,1)}, bf16[256,640]{1,0:T(8,128)(2,1)S(1)}, u32[]{:S(2)}, u32[]{:S(2)}) collective-permute-start(bf16[256,640]{1,0:T(8,128)(2,1)} %get-tuple-element.24), channel_id=1, source_target_pairs={{0,2},{2,4},{4,6},{6,7},{7,5},{5,3},{3,1},{1,0},{8,10},{10,12},{12... | collective-permute-start | bytes 983048 | tf_op jit(solution)/shard_map/ppermute | solution.py:181
  7.3 0.0 collective-permute-start.1
  7.3 2.2 %copy.18 = bf16[2048,1,192]{2,0,1:T(8,128)(2,1)} copy(bf16[2048,1,192]{0,2,1:T(8,128)(2,1)} %param.6) | data formatting | bytes 1572864 | tf_op args[0]
  9.5 0.7 %fusion.2 = (s32[8]{0:T(128)}, s32[8]{0:T(128)}) fusion(s32[4,512]{1,0:T(4,128)S(1)} %get-tuple-element.34, s32[4,512]{1,0:T(4,128)S(1)} %get-tuple-element.33), kind=kLoop, calls=%fused_computation.8 | loop fusion | flops 12272 | bytes 16448 | tf_op jit(solution)/shard_map/reduce_max | solution.py:218
  10.2 0.6 broadcast_select_fusion
  10.9 4.0 %collective-permute-done = bf16[256,640]{1,0:T(8,128)(2,1)S(1)} collective-permute-done((bf16[256,640]{1,0:T(8,128)(2,1)}, bf16[256,640]{1,0:T(8,128)(2,1)S(1)}, u32[]{:S(2)}, u32[]{:S(2)}) %collective-permute-start) | collective-permute-done | bytes 327712 | tf_op jit(solution)/shard_map/ppermute | solution.py:181
  14.8 0.9 %collective-permute-done.1 = bf16[256,640]{1,0:T(8,128)(2,1)S(1)} collective-permute-done((bf16[256,640]{1,0:T(8,128)(2,1)}, bf16[256,640]{1,0:T(8,128)(2,1)S(1)}, u32[]{:S(2)}, u32[]{:S(2)}) %collective-permute-start.1) | collective-permute-done | bytes 327712 | tf_op jit(solution)/shard_map/ppermute | solution.py:183
  15.7 1.3 %collective-permute-start.2 = (bf16[256,640]{1,0:T(8,128)(2,1)S(1)}, bf16[256,640]{1,0:T(8,128)(2,1)}, u32[]{:S(2)}, u32[]{:S(2)}) collective-permute-start(bf16[256,640]{1,0:T(8,128)(2,1)S(1)} %collective-permute-done), channel_id=1, source_target_pairs={{0,2},{2,4},{4,6},{6,7},{7,5},{5,3},{3,1},{1,0},{8,10},{10,12},{12... | collective-permute-start | bytes 983048 | tf_op jit(solution)/shard_map/ppermute | solution.py:181
  17.0 0.2 collective-permute-start.3
  21.5 1.6 %collective-permute-done.2 = bf16[256,640]{1,0:T(8,128)(2,1)} collective-permute-done((bf16[256,640]{1,0:T(8,128)(2,1)S(1)}, bf16[256,640]{1,0:T(8,128)(2,1)}, u32[]{:S(2)}, u32[]{:S(2)}) %collective-permute-start.2) | collective-permute-done | bytes 327712 | tf_op jit(solution)/shard_map/ppermute | solution.py:181
  23.2 1.3 %collective-permute-start.4 = (bf16[256,640]{1,0:T(8,128)(2,1)}, bf16[256,640]{1,0:T(8,128)(2,1)S(1)}, u32[]{:S(2)}, u32[]{:S(2)}) collective-permute-start(bf16[256,640]{1,0:T(8,128)(2,1)} %collective-permute-done.2), channel_id=1, source_target_pairs={{0,2},{2,4},{4,6},{6,7},{7,5},{5,3},{3,1},{1,0},{8,10},{10,12},{12... | collective-permute-start | bytes 983048 | tf_op jit(solution)/shard_map/ppermute | solution.py:181
  24.6 0.0 collective-permute-done.3
  24.6 0.2 collective-permute-start.5
  24.8 1.0 %constant_dynamic-update-slice_fusion.4 = bf16[2048,640]{1,0:T(8,128)(2,1)S(1)} fusion(bf16[2048,640]{1,0:T(8,128)(2,1)S(1)} %constant_dynamic-update-slice_fusion.5, bf16[256,640]{1,0:T(8,128)(2,1)} %collective-permute-done.2, s32[]{:T(128)S(6)} %select_n.55), kind=kLoop, calls=%fused_computation.18 | loop fusion | bytes 655364 | tf_op jit(solution)/shard_map/dynamic_update_slice | solution.py:192
  25.8 4.0 %collective-permute-done.4 = bf16[256,640]{1,0:T(8,128)(2,1)S(1)} collective-permute-done((bf16[256,640]{1,0:T(8,128)(2,1)}, bf16[256,640]{1,0:T(8,128)(2,1)S(1)}, u32[]{:S(2)}, u32[]{:S(2)}) %collective-permute-start.4) | collective-permute-done | bytes 327712 | tf_op jit(solution)/shard_map/ppermute | solution.py:181
  29.8 1.3 %collective-permute-start.6 = (bf16[256,640]{1,0:T(8,128)(2,1)S(1)}, bf16[256,640]{1,0:T(8,128)(2,1)S(1)}, u32[]{:S(2)}, u32[]{:S(2)}) collective-permute-start(bf16[256,640]{1,0:T(8,128)(2,1)S(1)} %collective-permute-done.4), channel_id=1, source_target_pairs={{0,2},{2,4},{4,6},{6,7},{7,5},{5,3},{3,1},{1,0},{8,10},{10,12},{12... | collective-permute-start | bytes 983048 | tf_op jit(solution)/shard_map/ppermute | solution.py:181
  31.1 1.0 %constant_dynamic-update-slice_fusion.3 = bf16[2048,640]{1,0:T(8,128)(2,1)S(1)} fusion(bf16[2048,640]{1,0:T(8,128)(2,1)S(1)} %constant_dynamic-update-slice_fusion.4, bf16[256,640]{1,0:T(8,128)(2,1)} %collective-permute-done.3, s32[]{:T(128)S(6)} %select_n.56), kind=kLoop, calls=%fused_computation.17 | loop fusion | bytes 655364 | tf_op jit(solution)/shard_map/dynamic_update_slice | solution.py:192
  32.2 0.0 collective-permute-done.5
  32.2 0.0 copy-start.4
  32.3 4.1 %collective-permute-done.6 = bf16[256,640]{1,0:T(8,128)(2,1)S(1)} collective-permute-done((bf16[256,640]{1,0:T(8,128)(2,1)S(1)}, bf16[256,640]{1,0:T(8,128)(2,1)S(1)}, u32[]{:S(2)}, u32[]{:S(2)}) %collective-permute-start.6) | collective-permute-done | bytes 327712 | tf_op jit(solution)/shard_map/ppermute | solution.py:181
  36.4 0.0 copy-done
  36.4 0.0 copy-start.3
  36.5 0.7 %convolution_convert_fusion = bf16[2048,128]{1,0:T(8,128)(2,1)S(1)} fusion(bf16[512,128]{1,0:T(8,128)(2,1)S(1)} %copy-done, bf16[2048,640]{1,0:T(8,128)(2,1)S(1)} %constant_dynamic-update-slice_fusion), kind=kOutput, calls=%fused_computation | convolution fusion | flops 268697600 | bytes 2752512 | tf_op jit(solution)/shard_map/dot_general | solution.py:228
  37.2 0.0 copy-done.4
  37.2 0.7 %convolution_convert_fusion.1 = bf16[2048,128]{1,0:T(8,128)(2,1)S(1)} fusion(bf16[512,128]{1,0:T(8,128)(2,1)S(1)} %copy-done.4, bf16[2048,640]{1,0:T(8,128)(2,1)S(1)} %constant_dynamic-update-slice_fusion), kind=kOutput, calls=%fused_computation.1 | convolution fusion | flops 268697600 | bytes 2752512 | tf_op jit(solution)/shard_map/dot_general | solution.py:225
  37.9 0.0 copy-done.3
  37.9 0.2 pad_maximum_fusion.rest_4_.rest_5_.rest_6_
  38.1 0.0 copy-start.1
  38.1 1.3 %collective-permute-start.7 = (bf16[2048,384]{1,0:T(8,128)(2,1)S(1)}, bf16[2048,384]{1,0:T(8,128)(2,1)S(1)}, u32[]{:S(2)}, u32[]{:S(2)}) collective-permute-start(bf16[2048,384]{1,0:T(8,128)(2,1)S(1)} %pad_maximum_fusion.rest_4_.rest_5_.rest_6_), channel_id=1, source_target_pairs={{0,8},{1,9},{2,10},{3,11},{4,12},{5,13},{6,14},{7,15},{16,24},{17,... | collective-permute-start | bytes 4718600 | tf_op jit(solution)/shard_map/ppermute | solution.py:243
  39.4 1.1 %slice.63 = bf16[4,1]{1,0:T(4,128)(2,1)S(1)} slice(bf16[2048,128]{1,0:T(8,128)(2,1)} %copy-done.3), slice={[511:2048:512], [64:65:1]} | slice | bytes 16 | tf_op jit(solution)/shard_map/slice | solution.py:237
  40.5 1.1 %slice.61 = bf16[4,1]{1,0:T(4,128)(2,1)S(1)} slice(bf16[2048,128]{1,0:T(8,128)(2,1)} %copy-done.3), slice={[0:2048:512], [64:65:1]} | slice | bytes 16 | tf_op jit(solution)/shard_map/slice | solution.py:236
  41.6 0.1 reduce.3
  41.8 0.1 reduce.1
  41.9 5.2 %collective-permute-done.7.rest_0_.rest_1_.rest_2_ = bf16[2048,384]{1,0:T(8,128)(2,1)S(1)} collective-permute-done((bf16[2048,384]{1,0:T(8,128)(2,1)S(1)}, bf16[2048,384]{1,0:T(8,128)(2,1)S(1)}, u32[]{:S(2)}, u32[]{:S(2)}) %collective-permute-start.7) | collective-permute-done | bytes 1572896 | tf_op jit(solution)/shard_map/ppermute | solution.py:243
  47.1 0.0 copy-start.2
  47.1 0.2 slice.62
  47.3 0.1 reduce.2
  47.4 0.2 slice.60
  47.6 0.1 reduce
  47.7 0.6 maximum_convert_fusion.1.kmaxd_ref
  48.3 0.6 maximum_convert_fusion.kmind_ref
  48.9 0.0 copy-done.1
  48.9 0.0 copy-done.2
  48.9 19.6 %shard_map.64 = bf16[2048,128]{1,0:T(8,128)(2,1)} custom-call(s32[1]{0:T(128)} %bitcast.qbase_ref, s32[8]{0:T(128)} %get-tuple-element.14.kminp_ref, s32[8]{0:T(128)} %get-tuple-element.15.kmaxp_ref, s32[8]{0:T(128)} %maximum_convert_fusion.kmind_ref, s32[8]{0:T(128)} %maximum_convert_fusion.1.kmaxd_ref, bf16[1,2048,192]{2,1,0:T(8,128)(2,1)} %bitcast.12, ...), custom_call_target="tpu_custom_call" | custom-call | tf_op jit(solution)/shard_map/pallas_call | solution.py:142
  (8 shorter events, 0.3 us)
Async XLA Ops:
  0.0 36.4 %copy-start = (bf16[512,128]{1,0:T(8,128)(2,1)S(1)}, bf16[512,128]{1,0:T(8,128)(2,1)}, u32[]{:S(2)}) copy-start(bf16[512,128]{1,0:T(8,128)(2,1)} %param.10) | copy-start | bytes 393220
  5.1 9.7 %collective-permute-start = (bf16[256,640]{1,0:T(8,128)(2,1)}, bf16[256,640]{1,0:T(8,128)(2,1)S(1)}, u32[]{:S(2)}, u32[]{:S(2)}) collective-permute-start(bf16[256,640]{1,0:T(8,128)(2,1)} %get-tuple-element.24), channel_id=1, source_target_pairs={{0,2},{2,4},{4,6},{6,7},{7,5},{5,3},{3,1},{1,0},{8,10},{10,12},{12... | collective-permute-start | bytes 983048 | tf_op jit(solution)/shard_map/ppermute | solution.py:181
  7.3 8.5 %collective-permute-start.1 = (bf16[256,640]{1,0:T(8,128)(2,1)}, bf16[256,640]{1,0:T(8,128)(2,1)S(1)}, u32[]{:S(2)}, u32[]{:S(2)}) collective-permute-start(bf16[256,640]{1,0:T(8,128)(2,1)} %get-tuple-element.24), channel_id=1, source_target_pairs={{2,0},{4,2},{6,4},{7,6},{5,7},{3,5},{1,3},{0,1},{10,8},{12,10},{14... | collective-permute-start | bytes 983048 | tf_op jit(solution)/shard_map/ppermute | solution.py:183
  15.7 7.4 %collective-permute-start.2 = (bf16[256,640]{1,0:T(8,128)(2,1)S(1)}, bf16[256,640]{1,0:T(8,128)(2,1)}, u32[]{:S(2)}, u32[]{:S(2)}) collective-permute-start(bf16[256,640]{1,0:T(8,128)(2,1)S(1)} %collective-permute-done), channel_id=1, source_target_pairs={{0,2},{2,4},{4,6},{6,7},{7,5},{5,3},{3,1},{1,0},{8,10},{10,12},{12... | collective-permute-start | bytes 983048 | tf_op jit(solution)/shard_map/ppermute | solution.py:181
  17.0 7.5 %collective-permute-start.3 = (bf16[256,640]{1,0:T(8,128)(2,1)S(1)}, bf16[256,640]{1,0:T(8,128)(2,1)}, u32[]{:S(2)}, u32[]{:S(2)}) collective-permute-start(bf16[256,640]{1,0:T(8,128)(2,1)S(1)} %collective-permute-done.1), channel_id=1, source_target_pairs={{2,0},{4,2},{6,4},{7,6},{5,7},{3,5},{1,3},{0,1},{10,8},{12,10},{14... | collective-permute-start | bytes 983048 | tf_op jit(solution)/shard_map/ppermute | solution.py:183
  23.2 6.6 %collective-permute-start.4 = (bf16[256,640]{1,0:T(8,128)(2,1)}, bf16[256,640]{1,0:T(8,128)(2,1)S(1)}, u32[]{:S(2)}, u32[]{:S(2)}) collective-permute-start(bf16[256,640]{1,0:T(8,128)(2,1)} %collective-permute-done.2), channel_id=1, source_target_pairs={{0,2},{2,4},{4,6},{6,7},{7,5},{5,3},{3,1},{1,0},{8,10},{10,12},{12... | collective-permute-start | bytes 983048 | tf_op jit(solution)/shard_map/ppermute | solution.py:181
  24.6 7.6 %collective-permute-start.5 = (bf16[256,640]{1,0:T(8,128)(2,1)}, bf16[256,640]{1,0:T(8,128)(2,1)S(1)}, u32[]{:S(2)}, u32[]{:S(2)}) collective-permute-start(bf16[256,640]{1,0:T(8,128)(2,1)} %collective-permute-done.3), channel_id=1, source_target_pairs={{2,0},{4,2},{6,4},{7,6},{5,7},{3,5},{1,3},{0,1},{10,8},{12,10},{14... | collective-permute-start | bytes 983048 | tf_op jit(solution)/shard_map/ppermute | solution.py:183
  29.8 6.5 %collective-permute-start.6 = (bf16[256,640]{1,0:T(8,128)(2,1)S(1)}, bf16[256,640]{1,0:T(8,128)(2,1)S(1)}, u32[]{:S(2)}, u32[]{:S(2)}) collective-permute-start(bf16[256,640]{1,0:T(8,128)(2,1)S(1)} %collective-permute-done.4), channel_id=1, source_target_pairs={{0,2},{2,4},{4,6},{6,7},{7,5},{5,3},{3,1},{1,0},{8,10},{10,12},{12... | collective-permute-start | bytes 983048 | tf_op jit(solution)/shard_map/ppermute | solution.py:181
  32.2 4.9 %copy-start.4 = (bf16[512,128]{1,0:T(8,128)(2,1)S(1)}, bf16[512,128]{1,0:T(8,128)(2,1)}, u32[]{:S(2)}) copy-start(bf16[512,128]{1,0:T(8,128)(2,1)} %param.9) | copy-start | bytes 393220
  36.4 1.4 %copy-start.3 = (bf16[2048,128]{1,0:T(8,128)(2,1)}, bf16[2048,128]{1,0:T(8,128)(2,1)S(1)}, u32[]{:S(2)}) copy-start(bf16[2048,128]{1,0:T(8,128)(2,1)S(1)} %slice.65) | copy-start | bytes 1572868
  38.1 10.8 %copy-start.1 = (bf16[2048,384]{1,0:T(8,128)(2,1)}, bf16[2048,384]{1,0:T(8,128)(2,1)S(1)}, u32[]{:S(2)}) copy-start(bf16[2048,384]{1,0:T(8,128)(2,1)S(1)} %pad_maximum_fusion.rest_4_.rest_5_.rest_6_) | copy-start | bytes 4718596
  38.1 9.0 %collective-permute-start.7 = (bf16[2048,384]{1,0:T(8,128)(2,1)S(1)}, bf16[2048,384]{1,0:T(8,128)(2,1)S(1)}, u32[]{:S(2)}, u32[]{:S(2)}) collective-permute-start(bf16[2048,384]{1,0:T(8,128)(2,1)S(1)} %pad_maximum_fusion.rest_4_.rest_5_.rest_6_), channel_id=1, source_target_pairs={{0,8},{1,9},{2,10},{3,11},{4,12},{5,13},{6,14},{7,15},{16,24},{17,... | collective-permute-start | bytes 4718600 | tf_op jit(solution)/shard_map/ppermute | solution.py:243
  47.1 1.8 %copy-start.2 = (bf16[2048,384]{1,0:T(8,128)(2,1)}, bf16[2048,384]{1,0:T(8,128)(2,1)S(1)}, u32[]{:S(2)}) copy-start(bf16[2048,384]{1,0:T(8,128)(2,1)S(1)} %collective-permute-done.7.rest_0_.rest_1_.rest_2_) | copy-start | bytes 4718596

commit v3 on v0

--- a/solution.py
+++ b/solution.py
@@ -188,8 +188,8 @@
             arrived.append(moving_b)
     rows = block.shape[0]
     placed = jnp.zeros((count * rows, block.shape[1]), block.dtype)
-    for number, piece in enumerate(arrived):
-        placed = lax.dynamic_update_slice(placed, piece, (source_of[number] * rows, 0))
+    for number in list(range(1, len(arrived))) + [0]:
+        placed = lax.dynamic_update_slice(placed, arrived[number], (source_of[number] * rows, 0))
     return placed, early
 
 

time: 67.3 us -> 65.8 us (0.978)
  the two profiles are of different devices: /device:TPU:1 before, /device:TPU:0 now
where the time goes in v3:
time: 65.8 us; the launch traced here: 65.4 us
  Pallas kernels  19.4 us (29%)
  waiting for transfers between devices  16.9 us (26%)
  starting transfers between devices  10.2 us (16%)
  local copies, waits for them, and re-layouts  8.11 us (12%)
  between operations  5.31 us (8%)
  other arithmetic  4.14 us (6%)
  matrix products  1.41 us (2%)
    pallas_call x1, Pallas kernels, flash(): pl.pallas_call(kernel, grid_spec=grid_spec, out_shape=jax.ShapeDtypeStruc...  19.4 us
    ppermute x4, waiting for transfers between devices, ring_gather(): moving_f = lax.ppermute(moving_f, 'tp', forward)  14.9 us
    ppermute x4, starting transfers between devices, ring_gather(): moving_f = lax.ppermute(moving_f, 'tp', forward)  7.86 us
    unnamed x12, local copies, waits for them, and re-layouts  3.45 us
    ppermute x3, waiting for transfers between devices, ring_gather(): moving_b = lax.ppermute(moving_b, 'tp', backward)  1.55 us
    ppermute x1, starting transfers between devices, body(): moved = lax.ppermute(pack, 'ctx', route)  1.39 us
  transfers between devices with their start and end apart: 8, of which 5 were waited for; matrix products, arithmetic and copies ran while one was open for 12% of the time, Pallas kernels for 0%

profile of v3, /device:TPU:0, one launch (start us, length us, event | category | flops | bytes accessed | tf_op | source)
XLA Modules:
  0.0 65.4 jit_solution(11934098161659477679)
XLA Ops:
  0.0 0.0 copy-start
  0.0 1.2 %copy.16 = bf16[256,576]{1,0:T(8,128)(2,1)S(1)} copy(bf16[256,576]{0,1:T(8,128)(2,1)} %param.7) | data formatting | bytes 589824 | tf_op args[1]
  1.2 0.7 %convert_element_type.25 = bf16[256]{0:T(256)(128)(2,1)S(1)} convert(s32[256]{0:T(256)} %param.8) | non-fusion elementwise | flops 256 | bytes 1536 | tf_op jit(solution)/shard_map/convert_element_type | solution.py:206
  1.9 0.1 broadcast_in_dim.20
  2.0 0.1 pad.11.clone
  2.1 0.1 maximum_maximum_fusion
  2.2 3.1 %collective-permute-start = (bf16[256,640]{1,0:T(8,128)(2,1)S(1)}, bf16[256,640]{1,0:T(8,128)(2,1)S(1)}, u32[]{:S(2)}, u32[]{:S(2)}) collective-permute-start(bf16[256,640]{1,0:T(8,128)(2,1)S(1)} %maximum_maximum_fusion), channel_id=1, source_target_pairs={{0,2},{2,4},{4,6},{6,7},{7,5},{5,3},{3,1},{1,0},{8,10},{10,12},{12... | collective-permute-start | bytes 983048 | tf_op jit(solution)/shard_map/ppermute | solution.py:181
  5.3 0.0 collective-permute-start.1
  5.3 2.2 %copy.18 = bf16[2048,1,192]{2,0,1:T(8,128)(2,1)} copy(bf16[2048,1,192]{0,2,1:T(8,128)(2,1)} %param.6) | data formatting | bytes 1572864 | tf_op args[0]
  7.5 0.7 %fusion.2 = (s32[8]{0:T(128)}, s32[8]{0:T(128)}) fusion(s32[4,512]{1,0:T(4,128)S(1)} %get-tuple-element.32, s32[4,512]{1,0:T(4,128)S(1)} %get-tuple-element.31), kind=kLoop, calls=%fused_computation.8 | loop fusion | flops 12272 | bytes 16448 | tf_op jit(solution)/shard_map/reduce_max | solution.py:218
  8.2 0.6 broadcast_select_fusion
  8.8 4.1 %collective-permute-done = bf16[256,640]{1,0:T(8,128)(2,1)S(1)} collective-permute-done((bf16[256,640]{1,0:T(8,128)(2,1)S(1)}, bf16[256,640]{1,0:T(8,128)(2,1)S(1)}, u32[]{:S(2)}, u32[]{:S(2)}) %collective-permute-start) | collective-permute-done | bytes 327712 | tf_op jit(solution)/shard_map/ppermute | solution.py:181
  12.9 1.5 %collective-permute-done.1 = bf16[256,640]{1,0:T(8,128)(2,1)S(1)} collective-permute-done((bf16[256,640]{1,0:T(8,128)(2,1)S(1)}, bf16[256,640]{1,0:T(8,128)(2,1)S(1)}, u32[]{:S(2)}, u32[]{:S(2)}) %collective-permute-start.1) | collective-permute-done | bytes 327712 | tf_op jit(solution)/shard_map/ppermute | solution.py:183
  14.4 1.6 %collective-permute-start.2 = (bf16[256,640]{1,0:T(8,128)(2,1)S(1)}, bf16[256,640]{1,0:T(8,128)(2,1)S(1)}, u32[]{:S(2)}, u32[]{:S(2)}) collective-permute-start(bf16[256,640]{1,0:T(8,128)(2,1)S(1)} %collective-permute-done), channel_id=1, source_target_pairs={{0,2},{2,4},{4,6},{6,7},{7,5},{5,3},{3,1},{1,0},{8,10},{10,12},{12... | collective-permute-start | bytes 983048 | tf_op jit(solution)/shard_map/ppermute | solution.py:181
  16.0 0.7 %constant_dynamic-slice_fusion = s32[1,8]{1,0:T(1,128)S(1)} fusion(s32[8,8]{1,0:T(8,128)} %constant.42.clone, s32[]{:T(128)S(6)} %select_n.51), kind=kLoop, calls=%fused_computation.22 | loop fusion | bytes 68 | tf_op jit(solution)/shard_map/dynamic_slice | solution.py:167
  16.7 0.4 collective-permute-start.3
  17.1 0.7 %fusion.5 = (s32[1,1]{1,0:T(1,128)}, s32[1,1]{1,0:T(1,128)}, s32[1,1]{1,0:T(1,128)}, s32[1,1]{1,0:T(1,128)}, s32[1,1]{1,0:T(1,128)}, /*index=5*/s32[1,1]{1,0:T(1,128)}, s32[1,1]{1,0:T(1,128)}, s32[1,1]{1,0:T(1,128)}) fusion(s32[1,8]{1,0:T(1,128)S(1)} %constant_dynamic-slice_fusion), kind=kLoop, calls=%fused_computation.25 | loop fusion | bytes 64 | tf_op jit(solution)/shard_map/slice | solution.py:192
  22.9 0.0 collective-permute-done.2
  22.9 1.6 %collective-permute-start.4 = (bf16[256,640]{1,0:T(8,128)(2,1)S(1)}, bf16[256,640]{1,0:T(8,128)(2,1)S(1)}, u32[]{:S(2)}, u32[]{:S(2)}) collective-permute-start(bf16[256,640]{1,0:T(8,128)(2,1)S(1)} %collective-permute-done.2), channel_id=1, source_target_pairs={{0,2},{2,4},{4,6},{6,7},{7,5},{5,3},{3,1},{1,0},{8,10},{10,12},{12... | collective-permute-start | bytes 983048 | tf_op jit(solution)/shard_map/ppermute | solution.py:181
  24.6 0.2 broadcast_in_dim.19
  24.9 0.0 collective-permute-done.3
  24.9 0.5 collective-permute-start.5
  25.4 5.4 %collective-permute-done.4 = bf16[256,640]{1,0:T(8,128)(2,1)S(1)} collective-permute-done((bf16[256,640]{1,0:T(8,128)(2,1)S(1)}, bf16[256,640]{1,0:T(8,128)(2,1)S(1)}, u32[]{:S(2)}, u32[]{:S(2)}) %collective-permute-start.4) | collective-permute-done | bytes 327712 | tf_op jit(solution)/shard_map/ppermute | solution.py:181
  30.9 1.6 %collective-permute-start.6 = (bf16[256,640]{1,0:T(8,128)(2,1)S(1)}, bf16[256,640]{1,0:T(8,128)(2,1)S(1)}, u32[]{:S(2)}, u32[]{:S(2)}) collective-permute-start(bf16[256,640]{1,0:T(8,128)(2,1)S(1)} %collective-permute-done.4), channel_id=1, source_target_pairs={{0,2},{2,4},{4,6},{6,7},{7,5},{5,3},{3,1},{1,0},{8,10},{10,12},{12... | collective-permute-start | bytes 983048 | tf_op jit(solution)/shard_map/ppermute | solution.py:181
  32.5 0.0 collective-permute-done.5
  32.6 5.3 %collective-permute-done.6 = bf16[256,640]{1,0:T(8,128)(2,1)S(1)} collective-permute-done((bf16[256,640]{1,0:T(8,128)(2,1)S(1)}, bf16[256,640]{1,0:T(8,128)(2,1)S(1)}, u32[]{:S(2)}, u32[]{:S(2)}) %collective-permute-start.6) | collective-permute-done | bytes 327712 | tf_op jit(solution)/shard_map/ppermute | solution.py:181
  38.0 0.0 copy-start.4
  38.0 0.1 constant_dynamic-update-slice_fusion
  38.2 0.0 copy-done
  38.2 0.0 copy-start.3
  38.2 0.7 %convolution_convert_fusion = bf16[2048,128]{1,0:T(8,128)(2,1)S(1)} fusion(bf16[512,128]{1,0:T(8,128)(2,1)S(1)} %copy-done, bf16[2048,640]{1,0:T(8,128)(2,1)S(1)} %constant_dynamic-update-slice_fusion), kind=kOutput, calls=%fused_computation | convolution fusion | flops 268697600 | bytes 2752512 | tf_op jit(solution)/shard_map/dot_general | solution.py:228
  38.9 0.0 copy-done.4
  38.9 0.7 %convolution_convert_fusion.1 = bf16[2048,128]{1,0:T(8,128)(2,1)S(1)} fusion(bf16[512,128]{1,0:T(8,128)(2,1)S(1)} %copy-done.4, bf16[2048,640]{1,0:T(8,128)(2,1)S(1)} %constant_dynamic-update-slice_fusion), kind=kOutput, calls=%fused_computation.1 | convolution fusion | flops 268697600 | bytes 2752512 | tf_op jit(solution)/shard_map/dot_general | solution.py:225
  39.6 0.0 copy-done.3
  39.6 0.2 pad_maximum_fusion.rest_4_.rest_5_.rest_6_
  39.8 0.0 copy-start.1
  39.8 1.4 %collective-permute-start.7 = (bf16[2048,384]{1,0:T(8,128)(2,1)S(1)}, bf16[2048,384]{1,0:T(8,128)(2,1)S(1)}, u32[]{:S(2)}, u32[]{:S(2)}) collective-permute-start(bf16[2048,384]{1,0:T(8,128)(2,1)S(1)} %pad_maximum_fusion.rest_4_.rest_5_.rest_6_), channel_id=1, source_target_pairs={{0,8},{1,9},{2,10},{3,11},{4,12},{5,13},{6,14},{7,15},{16,24},{17,... | collective-permute-start | bytes 4718600 | tf_op jit(solution)/shard_map/ppermute | solution.py:243
  41.2 1.1 %slice.63 = bf16[4,1]{1,0:T(4,128)(2,1)S(1)} slice(bf16[2048,128]{1,0:T(8,128)(2,1)} %copy-done.3), slice={[511:2048:512], [64:65:1]} | slice | bytes 16 | tf_op jit(solution)/shard_map/slice | solution.py:237
  42.3 1.1 %slice.61 = bf16[4,1]{1,0:T(4,128)(2,1)S(1)} slice(bf16[2048,128]{1,0:T(8,128)(2,1)} %copy-done.3), slice={[0:2048:512], [64:65:1]} | slice | bytes 16 | tf_op jit(solution)/shard_map/slice | solution.py:236
  43.5 0.1 reduce.3
  43.6 0.1 reduce.1
  43.7 0.5 collective-permute-done.7.rest_0_.rest_1_.rest_2_
  44.2 0.0 copy-start.2
  44.2 0.2 slice.62
  44.3 0.1 reduce.2
  44.5 0.2 slice.60
  44.6 0.1 reduce
  44.8 0.6 maximum_convert_fusion.1.kmaxd_ref
  45.4 0.7 maximum_convert_fusion.kmind_ref
  46.0 0.0 copy-done.1
  46.0 0.0 copy-done.2
  46.0 19.4 %shard_map.64 = bf16[2048,128]{1,0:T(8,128)(2,1)} custom-call(s32[1]{0:T(128)} %bitcast.qbase_ref, s32[8]{0:T(128)} %get-tuple-element.14.kminp_ref, s32[8]{0:T(128)} %get-tuple-element.15.kmaxp_ref, s32[8]{0:T(128)} %maximum_convert_fusion.kmind_ref, s32[8]{0:T(128)} %maximum_convert_fusion.1.kmaxd_ref, bf16[1,2048,192]{2,1,0:T(8,128)(2,1)} %bitcast.12, ...), custom_call_target="tpu_custom_call" | custom-call | tf_op jit(solution)/shard_map/pallas_call | solution.py:142
  (10 shorter events, 0.4 us)
Async XLA Ops:
  0.0 38.2 %copy-start = (bf16[512,128]{1,0:T(8,128)(2,1)S(1)}, bf16[512,128]{1,0:T(8,128)(2,1)}, u32[]{:S(2)}) copy-start(bf16[512,128]{1,0:T(8,128)(2,1)} %param.10) | copy-start | bytes 393220
  2.2 10.7 %collective-permute-start = (bf16[256,640]{1,0:T(8,128)(2,1)S(1)}, bf16[256,640]{1,0:T(8,128)(2,1)S(1)}, u32[]{:S(2)}, u32[]{:S(2)}) collective-permute-start(bf16[256,640]{1,0:T(8,128)(2,1)S(1)} %maximum_maximum_fusion), channel_id=1, source_target_pairs={{0,2},{2,4},{4,6},{6,7},{7,5},{5,3},{3,1},{1,0},{8,10},{10,12},{12... | collective-permute-start | bytes 983048 | tf_op jit(solution)/shard_map/ppermute | solution.py:181
  5.3 9.2 %collective-permute-start.1 = (bf16[256,640]{1,0:T(8,128)(2,1)S(1)}, bf16[256,640]{1,0:T(8,128)(2,1)S(1)}, u32[]{:S(2)}, u32[]{:S(2)}) collective-permute-start(bf16[256,640]{1,0:T(8,128)(2,1)S(1)} %maximum_maximum_fusion), channel_id=1, source_target_pairs={{2,0},{4,2},{6,4},{7,6},{5,7},{3,5},{1,3},{0,1},{10,8},{12,10},{14... | collective-permute-start | bytes 983048 | tf_op jit(solution)/shard_map/ppermute | solution.py:183
  14.4 8.5 %collective-permute-start.2 = (bf16[256,640]{1,0:T(8,128)(2,1)S(1)}, bf16[256,640]{1,0:T(8,128)(2,1)S(1)}, u32[]{:S(2)}, u32[]{:S(2)}) collective-permute-start(bf16[256,640]{1,0:T(8,128)(2,1)S(1)} %collective-permute-done), channel_id=1, source_target_pairs={{0,2},{2,4},{4,6},{6,7},{7,5},{5,3},{3,1},{1,0},{8,10},{10,12},{12... | collective-permute-start | bytes 983048 | tf_op jit(solution)/shard_map/ppermute | solution.py:181
  16.7 8.2 %collective-permute-start.3 = (bf16[256,640]{1,0:T(8,128)(2,1)S(1)}, bf16[256,640]{1,0:T(8,128)(2,1)S(1)}, u32[]{:S(2)}, u32[]{:S(2)}) collective-permute-start(bf16[256,640]{1,0:T(8,128)(2,1)S(1)} %collective-permute-done.1), channel_id=1, source_target_pairs={{2,0},{4,2},{6,4},{7,6},{5,7},{3,5},{1,3},{0,1},{10,8},{12,10},{14... | collective-permute-start | bytes 983048 | tf_op jit(solution)/shard_map/ppermute | solution.py:183
  22.9 7.9 %collective-permute-start.4 = (bf16[256,640]{1,0:T(8,128)(2,1)S(1)}, bf16[256,640]{1,0:T(8,128)(2,1)S(1)}, u32[]{:S(2)}, u32[]{:S(2)}) collective-permute-start(bf16[256,640]{1,0:T(8,128)(2,1)S(1)} %collective-permute-done.2), channel_id=1, source_target_pairs={{0,2},{2,4},{4,6},{6,7},{7,5},{5,3},{3,1},{1,0},{8,10},{10,12},{12... | collective-permute-start | bytes 983048 | tf_op jit(solution)/shard_map/ppermute | solution.py:181
  24.9 7.6 %collective-permute-start.5 = (bf16[256,640]{1,0:T(8,128)(2,1)S(1)}, bf16[256,640]{1,0:T(8,128)(2,1)S(1)}, u32[]{:S(2)}, u32[]{:S(2)}) collective-permute-start(bf16[256,640]{1,0:T(8,128)(2,1)S(1)} %collective-permute-done.3), channel_id=1, source_target_pairs={{2,0},{4,2},{6,4},{7,6},{5,7},{3,5},{1,3},{0,1},{10,8},{12,10},{14... | collective-permute-start | bytes 983048 | tf_op jit(solution)/shard_map/ppermute | solution.py:183
  30.9 7.1 %collective-permute-start.6 = (bf16[256,640]{1,0:T(8,128)(2,1)S(1)}, bf16[256,640]{1,0:T(8,128)(2,1)S(1)}, u32[]{:S(2)}, u32[]{:S(2)}) collective-permute-start(bf16[256,640]{1,0:T(8,128)(2,1)S(1)} %collective-permute-done.4), channel_id=1, source_target_pairs={{0,2},{2,4},{4,6},{6,7},{7,5},{5,3},{3,1},{1,0},{8,10},{10,12},{12... | collective-permute-start | bytes 983048 | tf_op jit(solution)/shard_map/ppermute | solution.py:181
  38.0 0.9 %copy-start.4 = (bf16[512,128]{1,0:T(8,128)(2,1)S(1)}, bf16[512,128]{1,0:T(8,128)(2,1)}, u32[]{:S(2)}) copy-start(bf16[512,128]{1,0:T(8,128)(2,1)} %param.9) | copy-start | bytes 393220
  38.2 1.4 %copy-start.3 = (bf16[2048,128]{1,0:T(8,128)(2,1)}, bf16[2048,128]{1,0:T(8,128)(2,1)S(1)}, u32[]{:S(2)}) copy-start(bf16[2048,128]{1,0:T(8,128)(2,1)S(1)} %slice.65) | copy-start | bytes 1572868
  39.8 6.2 %copy-start.1 = (bf16[2048,384]{1,0:T(8,128)(2,1)}, bf16[2048,384]{1,0:T(8,128)(2,1)S(1)}, u32[]{:S(2)}) copy-start(bf16[2048,384]{1,0:T(8,128)(2,1)S(1)} %pad_maximum_fusion.rest_4_.rest_5_.rest_6_) | copy-start | bytes 4718596
  39.8 4.3 %collective-permute-start.7 = (bf16[2048,384]{1,0:T(8,128)(2,1)S(1)}, bf16[2048,384]{1,0:T(8,128)(2,1)S(1)}, u32[]{:S(2)}, u32[]{:S(2)}) collective-permute-start(bf16[2048,384]{1,0:T(8,128)(2,1)S(1)} %pad_maximum_fusion.rest_4_.rest_5_.rest_6_), channel_id=1, source_target_pairs={{0,8},{1,9},{2,10},{3,11},{4,12},{5,13},{6,14},{7,15},{16,24},{17,... | collective-permute-start | bytes 4718600 | tf_op jit(solution)/shard_map/ppermute | solution.py:243
  44.2 1.9 %copy-start.2 = (bf16[2048,384]{1,0:T(8,128)(2,1)}, bf16[2048,384]{1,0:T(8,128)(2,1)S(1)}, u32[]{:S(2)}) copy-start(bf16[2048,384]{1,0:T(8,128)(2,1)S(1)} %collective-permute-done.7.rest_0_.rest_1_.rest_2_) | copy-start | bytes 4718596
